TPU v7x, 128 devices: a whole 4x4x4 slice. The times are simulated.
128 devices in a mesh: wide: 16 (over y, x), narrow: 8 (over z, core).
Axes of the slice: x: 4, y: 4, z: 4, core: 2. Of those that a mesh axis runs over, the one named last changes fastest.
Arguments:
- x_rows: float32 [65536, 256], P('wide'), may hold values from -1.5 to 1.5
- y_cols: float32 [131072, 256], P(('wide', 'narrow')), may hold values from -1.5 to 1.5
- tile_values: bfloat16 [16, 8, 256, 128, 128], P('wide', 'narrow'), may hold values from -6 to 6
- tile_row: int32 [16, 8, 256], P('wide', 'narrow'), may hold values from 0 to 31, as said below
- tile_col: int32 [16, 8, 256], P('wide', 'narrow'), may hold values from 0 to 127
- tile_count: int32 [16, 8], P('wide', 'narrow'), may hold values from 32 to 256, as said below
Outputs:
- x_new: float32 [65536, 256], P('wide')
- y_new: float32 [131072, 256], P(('wide', 'narrow'))
Inputs may be any that keep to these rules, and one draw needn't show every extreme that they name: On each device the (tile_row, tile_col) pairs of all 256 slots are distinct. `tile_count`: some device has all 256 slots live.
All inputs are finite; a program needn't handle non-finite values.
Results may differ from a plain program's by a relative error of at most 0.017.
Values may be sent and summed in bfloat16 or wider, within the bound.
No kernel may reach another device: no remote copies, remote signals or barrier semaphores. Data moves between devices by JAX's collectives and lax.ppermute only.
A program may use at most 192 MiB of HBM per device.

v0:
```python
import jax
import jax.numpy as jnp
from jax import lax
from jax.sharding import PartitionSpec as P

huber_delta = 1.0
step_rows = 0.008
penalty = 3.0
step_columns = 0.012


def shrink(value, level):
    return jnp.sign(value) * jnp.maximum(jnp.abs(value) - level, 0.0)


def one_hot(index, count):
    return (index[:, None] == jnp.arange(count, dtype=jnp.int32)[None, :]).astype(jnp.bfloat16)


def pick_rows(table, flat):
    return jnp.dot(table, flat, preferred_element_type=jnp.float32).astype(jnp.bfloat16)


def spread_add(acc, table, contrib):
    upper = contrib.astype(jnp.bfloat16)
    remain = contrib - upper.astype(jnp.float32)
    middle = remain.astype(jnp.bfloat16)
    lower = (remain - middle.astype(jnp.float32)).astype(jnp.bfloat16)
    dims = (((0,), (0,)), ((), ()))
    for piece in (upper, middle, lower):
        acc = acc + lax.dot_general(table, piece, dims, preferred_element_type=jnp.float32)
    return acc


def shards(x_rows, y_cols, tile_values, tile_row, tile_col, tile_count):
    slots = tile_row.shape[-1]
    tile = tile_values.shape[-1]
    rank = x_rows.shape[1]
    row_blocks = x_rows.shape[0] // tile
    y_part = lax.all_gather(y_cols.astype(jnp.bfloat16), "wide", axis=0, tiled=True)
    col_blocks = y_part.shape[0] // tile
    y_flat = y_part.reshape(col_blocks, tile * rank)
    values = tile_values.reshape(slots, tile, tile)
    rows_index = tile_row.reshape(slots)
    cols_index = tile_col.reshape(slots)
    filled = tile_count.reshape(())
    width = min(64, slots)
    y_slots = pick_rows(one_hot(cols_index, col_blocks), y_flat)

    def sweep(x_blocks, want_rows):
        segments = row_blocks if want_rows else col_blocks
        x_flat = x_blocks.reshape(row_blocks, tile * rank)

        def visit(turn, acc):
            start = turn * width
            rows_here = lax.dynamic_slice_in_dim(rows_index, start, width)
            cols_here = lax.dynamic_slice_in_dim(cols_index, start, width)
            vals = lax.dynamic_slice_in_dim(values, start, width, 0)
            live = (start + jnp.arange(width, dtype=jnp.int32) < filled).astype(jnp.float32)
            row_table = one_hot(rows_here, row_blocks)
            xs = pick_rows(row_table, x_flat).reshape(width, tile, rank)
            ys = lax.dynamic_slice_in_dim(y_slots, start, width, 0).reshape(width, tile, rank)
            pred = jnp.einsum("gik,gjk->gij", xs, ys, preferred_element_type=jnp.float32)
            slope = (
                jnp.clip(pred - vals.astype(jnp.float32), -huber_delta, huber_delta)
                * live[:, None, None]
            ).astype(jnp.bfloat16)
            if want_rows:
                contrib = jnp.einsum("gij,gjk->gik", slope, ys, preferred_element_type=jnp.float32)
                table = row_table
            else:
                contrib = jnp.einsum("gij,gik->gjk", slope, xs, preferred_element_type=jnp.float32)
                table = one_hot(cols_here, col_blocks)
            return spread_add(acc, table, contrib.reshape(width, tile * rank))

        init = jnp.zeros((segments, tile * rank), jnp.float32)
        turns = slots // width
        return lax.fori_loop(0, turns, visit, init)

    x_now = x_rows
    for turn in range(2):
        x_blocks = x_now.astype(jnp.bfloat16).reshape(row_blocks, tile, rank)
        partial_rows = sweep(x_blocks, True).reshape(x_now.shape)
        grad_x = lax.psum(partial_rows, "narrow")
        x_now = shrink(x_now - step_rows * grad_x, step_rows * penalty)
    x_blocks = x_now.astype(jnp.bfloat16).reshape(row_blocks, tile, rank)
    partial_cols = sweep(x_blocks, False).reshape(col_blocks * tile, rank)
    grad_y = lax.psum_scatter(partial_cols, "wide", scatter_dimension=0, tiled=True)
    return (x_now, y_cols - step_columns * grad_y)


def solution(mesh):
    placed = (
        P("wide", None),
        P(("wide", "narrow"), None),
        P("wide", "narrow", None, None, None),
        P("wide", "narrow", None),
        P("wide", "narrow", None),
        P("wide", "narrow"),
    )
    return jax.shard_map(
        shards,
        mesh=mesh,
        in_specs=placed,
        out_specs=(P("wide", None), P(("wide", "narrow"), None)),
        check_vma=False,
    )
```

profile of v0, /device:TPU:0, one launch (start us, length us, event | category | flops | bytes accessed | tf_op | source)
XLA Modules:
  0.0 976.2 jit_solution(1666042726776238650)
XLA Ops:
  16.0 67.9 %all-gather.2.cloned.1.call-done = bf16[16384,256]{1,0:T(8,128)(2,1)} async-done(((bf16[1024,256]{1,0:T(8,128)(2,1)}), bf16[16384,256]{1,0:T(8,128)(2,1)}) %all-gather.2.cloned.1.call-update) | async-done | bytes 8388624 | tf_op jit(solution)/shard_map/all_gather | solution.py:40
  83.9 13.5 %reshape.113 = bf16[128,32768]{1,0:T(8,128)(2,1)} reshape(bf16[16384,256]{1,0:T(8,128)(2,1)} %all-gather.2.cloned.1.call-done) | data formatting | bytes 16777216 | tf_op jit(solution)/shard_map/reshape | solution.py:42
  97.4 11.5 %convolution_convert_fusion.3 = bf16[256,32768]{1,0:T(8,128)(2,1)} fusion(bf16[128,32768]{1,0:T(8,128)(2,1)} %reshape.113, s32[256]{0:T(256)S(1)} %bitcast.124), kind=kOutput, calls=%fused_computation.61 | convolution fusion | flops 2155905024 | bytes 25166848 | tf_op jit(solution)/shard_map/dot_general | solution.py:21
  108.9 139.2 %while.42 = (s32[]{:T(128)}, f32[32,32768]{1,0:T(8,128)}, s32[256]{0:T(256)S(1)}, bf16[32,32768]{1,0:T(8,128)(2,1)S(1)}, bf16[256,32768]{1,0:T(8,128)(2,1)}, /*i...) while((s32[]{:T(128)}, f32[32,32768]{1,0:T(8,128)}, ...), condition=%wide.region_1.2_spmd.clone, body=%wide.region_0.1_spmd.clone.sunk | while | flops 1647321344 | bytes 138414320 | solution.py:78
  119.6 10.9 %fusion.76 = f32[64,128,256]{2,1,0:T(8,128)} fusion(bf16[64,128,256]{2,1,0:T(8,128)(2,1)} %bitcast.107, bf16[64,128,256]{2,1,0:T(8,128)(2,1)} %bitcast.118, f32[64]{0:T(128)S(1)} %compare_convert_fusion.6, bf16[256,128,128]{2,1,0:T(8,128)(2,1)} %get-tuple-element.689, s32[]{:T(128)S(6)} %select_n.34), kind=kOutput, calls=%fused_computation.9.clone.1 | convolution fusion | flops 1078984704 | bytes 23068932 | tf_op jit(solution)/shard_map/while/body/eval_jaxpr/gij,gjk->gik/dot_general | solution.py:69
  130.5 8.3 copy.33
  154.4 10.9 %fusion.76 = f32[64,128,256]{2,1,0:T(8,128)} fusion(bf16[64,128,256]{2,1,0:T(8,128)(2,1)} %bitcast.107, bf16[64,128,256]{2,1,0:T(8,128)(2,1)} %bitcast.118, f32[64]{0:T(128)S(1)} %compare_convert_fusion.6, bf16[256,128,128]{2,1,0:T(8,128)(2,1)} %get-tuple-element.689, s32[]{:T(128)S(6)} %select_n.34), kind=kOutput, calls=%fused_computation.9.clone.1 | convolution fusion | flops 1078984704 | bytes 23068932 | tf_op jit(solution)/shard_map/while/body/eval_jaxpr/gij,gjk->gik/dot_general | solution.py:69
  165.2 8.3 copy.33
  189.1 10.9 %fusion.76 = f32[64,128,256]{2,1,0:T(8,128)} fusion(bf16[64,128,256]{2,1,0:T(8,128)(2,1)} %bitcast.107, bf16[64,128,256]{2,1,0:T(8,128)(2,1)} %bitcast.118, f32[64]{0:T(128)S(1)} %compare_convert_fusion.6, bf16[256,128,128]{2,1,0:T(8,128)(2,1)} %get-tuple-element.689, s32[]{:T(128)S(6)} %select_n.34), kind=kOutput, calls=%fused_computation.9.clone.1 | convolution fusion | flops 1078984704 | bytes 23068932 | tf_op jit(solution)/shard_map/while/body/eval_jaxpr/gij,gjk->gik/dot_general | solution.py:69
  200.0 8.3 copy.33
  223.9 10.9 %fusion.76 = f32[64,128,256]{2,1,0:T(8,128)} fusion(bf16[64,128,256]{2,1,0:T(8,128)(2,1)} %bitcast.107, bf16[64,128,256]{2,1,0:T(8,128)(2,1)} %bitcast.118, f32[64]{0:T(128)S(1)} %compare_convert_fusion.6, bf16[256,128,128]{2,1,0:T(8,128)(2,1)} %get-tuple-element.689, s32[]{:T(128)S(6)} %select_n.34), kind=kOutput, calls=%fused_computation.9.clone.1 | convolution fusion | flops 1078984704 | bytes 23068932 | tf_op jit(solution)/shard_map/while/body/eval_jaxpr/gij,gjk->gik/dot_general | solution.py:69
  234.8 8.3 copy.33
  253.1 72.4 %all-reduce.3.cloned.1.call-done = f32[4096,256]{1,0:T(8,128)} async-done(((f32[4096,256]{1,0:T(8,128)}), f32[4096,256]{1,0:T(8,128)}) %all-reduce.3.cloned.1.call-update) | async-done | bytes 4194320 | tf_op jit(solution)/shard_map/psum | solution.py:84
  335.0 139.6 %while.43 = (s32[]{:T(128)}, f32[32,32768]{1,0:T(8,128)}, s32[256]{0:T(256)S(1)}, bf16[32,32768]{1,0:T(8,128)(2,1)S(1)}, bf16[256,32768]{1,0:T(8,128)(2,1)}, /*i...) while((s32[]{:T(128)}, f32[32,32768]{1,0:T(8,128)}, ...), condition=%wide.region_4.5_spmd.clone, body=%wide.region_3.4_spmd.clone.sunk | while | flops 1647321344 | bytes 138414320 | solution.py:78
  346.0 10.8 %fusion.83 = f32[64,128,256]{2,1,0:T(8,128)} fusion(bf16[64,128,256]{2,1,0:T(8,128)(2,1)} %bitcast.108, bf16[64,128,256]{2,1,0:T(8,128)(2,1)} %bitcast.119, f32[64]{0:T(128)S(1)} %compare_convert_fusion.7, bf16[256,128,128]{2,1,0:T(8,128)(2,1)} %get-tuple-element.722, s32[]{:T(128)S(6)} %select_n.35), kind=kOutput, calls=%fused_computation.29.clone.1 | convolution fusion | flops 1078984704 | bytes 23068932 | tf_op jit(solution)/shard_map/while/body/eval_jaxpr/gij,gjk->gik/dot_general | solution.py:69
  356.8 8.3 copy.36
  380.7 10.9 %fusion.83 = f32[64,128,256]{2,1,0:T(8,128)} fusion(bf16[64,128,256]{2,1,0:T(8,128)(2,1)} %bitcast.108, bf16[64,128,256]{2,1,0:T(8,128)(2,1)} %bitcast.119, f32[64]{0:T(128)S(1)} %compare_convert_fusion.7, bf16[256,128,128]{2,1,0:T(8,128)(2,1)} %get-tuple-element.722, s32[]{:T(128)S(6)} %select_n.35), kind=kOutput, calls=%fused_computation.29.clone.1 | convolution fusion | flops 1078984704 | bytes 23068932 | tf_op jit(solution)/shard_map/while/body/eval_jaxpr/gij,gjk->gik/dot_general | solution.py:69
  391.6 8.3 copy.36
  415.5 10.9 %fusion.83 = f32[64,128,256]{2,1,0:T(8,128)} fusion(bf16[64,128,256]{2,1,0:T(8,128)(2,1)} %bitcast.108, bf16[64,128,256]{2,1,0:T(8,128)(2,1)} %bitcast.119, f32[64]{0:T(128)S(1)} %compare_convert_fusion.7, bf16[256,128,128]{2,1,0:T(8,128)(2,1)} %get-tuple-element.722, s32[]{:T(128)S(6)} %select_n.35), kind=kOutput, calls=%fused_computation.29.clone.1 | convolution fusion | flops 1078984704 | bytes 23068932 | tf_op jit(solution)/shard_map/while/body/eval_jaxpr/gij,gjk->gik/dot_general | solution.py:69
  426.3 8.3 copy.36
  450.2 10.8 %fusion.83 = f32[64,128,256]{2,1,0:T(8,128)} fusion(bf16[64,128,256]{2,1,0:T(8,128)(2,1)} %bitcast.108, bf16[64,128,256]{2,1,0:T(8,128)(2,1)} %bitcast.119, f32[64]{0:T(128)S(1)} %compare_convert_fusion.7, bf16[256,128,128]{2,1,0:T(8,128)(2,1)} %get-tuple-element.722, s32[]{:T(128)S(6)} %select_n.35), kind=kOutput, calls=%fused_computation.29.clone.1 | convolution fusion | flops 1078984704 | bytes 23068932 | tf_op jit(solution)/shard_map/while/body/eval_jaxpr/gij,gjk->gik/dot_general | solution.py:69
  461.1 8.3 copy.36
  479.5 12.0 %copy.8 = bf16[1,1,256,128,128]{3,4,2,1,0:T(8,128)(2,1)} copy(bf16[1,1,256,128,128]{4,3,2,1,0:T(8,128)(2,1)} %bitcast.122) | data formatting | bytes 16777216 | tf_op args[2]
  491.5 60.7 %all-reduce.5.cloned.1.call-done = f32[4096,256]{1,0:T(8,128)} async-done(((f32[4096,256]{1,0:T(8,128)}), f32[4096,256]{1,0:T(8,128)}) %all-reduce.5.cloned.1.call-update) | async-done | bytes 4194320 | tf_op jit(solution)/shard_map/psum | solution.py:84
  552.3 10.3 %fusion.35 = (bf16[4096,256]{1,0:T(8,128)(2,1)S(1)}, f32[4096,256]{1,0:T(8,128)}) fusion(f32[4096,256]{1,0:T(8,128)} %all-reduce.5.cloned.1.call-done, f32[4096,256]{1,0:T(8,128)} %param.12, f32[4096,256]{1,0:T(8,128)} %all-reduce.3.cloned.1.call-done), kind=kLoop, calls=%fused_computation.68 | loop fusion | flops 15728640 | bytes 18874368 | tf_op jit(solution)/shard_map/convert_element_type | solution.py:86
  564.9 273.5 %while.44 = (s32[]{:T(128)}, f32[128,32768]{1,0:T(8,128)}, s32[256]{0:T(256)S(1)}, s32[256]{0:T(256)S(1)}, bf16[32,32768]{1,0:T(8,128)(2,1)}, /*index=5*/bf16[25...) while((s32[]{:T(128)}, f32[128,32768]{1,0:T(8,128)}, ...), condition=%wide.region_7.8_spmd.clone, body=%wide.region_6.7_spmd.clone.sunk | while | flops 2867882240 | bytes 197135056 | solution.py:78
  577.1 10.8 %fusion.90 = f32[64,128,256]{2,1,0:T(8,128)} fusion(bf16[64,128,256]{2,1,0:T(8,128)(2,1)} %bitcast.106, bf16[64,128,256]{2,1,0:T(8,128)(2,1)} %bitcast.120, f32[64]{0:T(128)S(1)} %compare_convert_fusion.8, bf16[256,128,128]{1,2,0:T(8,128)(2,1)} %get-tuple-element.758, s32[]{:T(128)S(6)} %select_n.36), kind=kOutput, calls=%fused_computation.49.clone.1 | convolution fusion | flops 1078984704 | bytes 23068932 | tf_op jit(solution)/shard_map/while/body/eval_jaxpr/gij,gik->gjk/dot_general | solution.py:72
  587.9 8.1 copy.39
  596.0 8.3 convolution_add_fusion.24
  604.4 14.0 %convolution_add_fusion.25 = f32[128,32768]{1,0:T(8,128)} fusion(f32[128,32768]{1,0:T(8,128)} %convolution_add_fusion.24, f32[64,32768]{1,0:T(8,128)S(1)} %bitcast.104, s32[64]{0:T(128)S(1)} %dynamic_slice.111), kind=kOutput, calls=%fused_computation.41.clone.1 | convolution fusion | flops 549462016 | bytes 41943296 | tf_op jit(solution)/shard_map/while/body/eval_jaxpr/dot_general | solution.py:31
  618.4 10.6 %convolution_add_fusion.26 = f32[128,32768]{1,0:T(8,128)} fusion(f32[128,32768]{1,0:T(8,128)} %convolution_add_fusion.25, f32[64,32768]{1,0:T(8,128)S(1)} %bitcast.105, s32[64]{0:T(128)S(1)} %dynamic_slice.111), kind=kOutput, calls=%fused_computation.40.clone.1 | convolution fusion | flops 555753472 | bytes 41943296 | tf_op jit(solution)/shard_map/while/body/eval_jaxpr/dot_general | solution.py:31
  641.1 10.8 %fusion.90 = f32[64,128,256]{2,1,0:T(8,128)} fusion(bf16[64,128,256]{2,1,0:T(8,128)(2,1)} %bitcast.106, bf16[64,128,256]{2,1,0:T(8,128)(2,1)} %bitcast.120, f32[64]{0:T(128)S(1)} %compare_convert_fusion.8, bf16[256,128,128]{1,2,0:T(8,128)(2,1)} %get-tuple-element.758, s32[]{:T(128)S(6)} %select_n.36), kind=kOutput, calls=%fused_computation.49.clone.1 | convolution fusion | flops 1078984704 | bytes 23068932 | tf_op jit(solution)/shard_map/while/body/eval_jaxpr/gij,gik->gjk/dot_general | solution.py:72
  652.0 8.1 copy.39
  660.1 14.1 %convolution_add_fusion.24 = f32[128,32768]{1,0:T(8,128)} fusion(f32[128,32768]{1,0:T(8,128)} %get-tuple-element.741, pred[]{:T(512)S(6)} %compare.11, f32[64,32768]{1,0:T(8,128)S(1)} %bitcast.103, s32[64]{0:T(128)S(1)} %dynamic_slice.111), kind=kOutput, calls=%fused_computation.42.clone.1 | convolution fusion | flops 547364864 | bytes 41943296 | tf_op jit(solution)/shard_map/while/body/eval_jaxpr/dot_general | solution.py:31
  674.2 14.0 %convolution_add_fusion.25 = f32[128,32768]{1,0:T(8,128)} fusion(f32[128,32768]{1,0:T(8,128)} %convolution_add_fusion.24, f32[64,32768]{1,0:T(8,128)S(1)} %bitcast.104, s32[64]{0:T(128)S(1)} %dynamic_slice.111), kind=kOutput, calls=%fused_computation.41.clone.1 | convolution fusion | flops 549462016 | bytes 41943296 | tf_op jit(solution)/shard_map/while/body/eval_jaxpr/dot_general | solution.py:31
  688.2 10.6 %convolution_add_fusion.26 = f32[128,32768]{1,0:T(8,128)} fusion(f32[128,32768]{1,0:T(8,128)} %convolution_add_fusion.25, f32[64,32768]{1,0:T(8,128)S(1)} %bitcast.105, s32[64]{0:T(128)S(1)} %dynamic_slice.111), kind=kOutput, calls=%fused_computation.40.clone.1 | convolution fusion | flops 555753472 | bytes 41943296 | tf_op jit(solution)/shard_map/while/body/eval_jaxpr/dot_general | solution.py:31
  711.0 10.8 %fusion.90 = f32[64,128,256]{2,1,0:T(8,128)} fusion(bf16[64,128,256]{2,1,0:T(8,128)(2,1)} %bitcast.106, bf16[64,128,256]{2,1,0:T(8,128)(2,1)} %bitcast.120, f32[64]{0:T(128)S(1)} %compare_convert_fusion.8, bf16[256,128,128]{1,2,0:T(8,128)(2,1)} %get-tuple-element.758, s32[]{:T(128)S(6)} %select_n.36), kind=kOutput, calls=%fused_computation.49.clone.1 | convolution fusion | flops 1078984704 | bytes 23068932 | tf_op jit(solution)/shard_map/while/body/eval_jaxpr/gij,gik->gjk/dot_general | solution.py:72
  721.8 8.1 copy.39
  729.9 14.1 %convolution_add_fusion.24 = f32[128,32768]{1,0:T(8,128)} fusion(f32[128,32768]{1,0:T(8,128)} %get-tuple-element.741, pred[]{:T(512)S(6)} %compare.11, f32[64,32768]{1,0:T(8,128)S(1)} %bitcast.103, s32[64]{0:T(128)S(1)} %dynamic_slice.111), kind=kOutput, calls=%fused_computation.42.clone.1 | convolution fusion | flops 547364864 | bytes 41943296 | tf_op jit(solution)/shard_map/while/body/eval_jaxpr/dot_general | solution.py:31
  744.0 14.0 %convolution_add_fusion.25 = f32[128,32768]{1,0:T(8,128)} fusion(f32[128,32768]{1,0:T(8,128)} %convolution_add_fusion.24, f32[64,32768]{1,0:T(8,128)S(1)} %bitcast.104, s32[64]{0:T(128)S(1)} %dynamic_slice.111), kind=kOutput, calls=%fused_computation.41.clone.1 | convolution fusion | flops 549462016 | bytes 41943296 | tf_op jit(solution)/shard_map/while/body/eval_jaxpr/dot_general | solution.py:31
  758.0 10.6 %convolution_add_fusion.26 = f32[128,32768]{1,0:T(8,128)} fusion(f32[128,32768]{1,0:T(8,128)} %convolution_add_fusion.25, f32[64,32768]{1,0:T(8,128)S(1)} %bitcast.105, s32[64]{0:T(128)S(1)} %dynamic_slice.111), kind=kOutput, calls=%fused_computation.40.clone.1 | convolution fusion | flops 555753472 | bytes 41943296 | tf_op jit(solution)/shard_map/while/body/eval_jaxpr/dot_general | solution.py:31
  780.8 10.8 %fusion.90 = f32[64,128,256]{2,1,0:T(8,128)} fusion(bf16[64,128,256]{2,1,0:T(8,128)(2,1)} %bitcast.106, bf16[64,128,256]{2,1,0:T(8,128)(2,1)} %bitcast.120, f32[64]{0:T(128)S(1)} %compare_convert_fusion.8, bf16[256,128,128]{1,2,0:T(8,128)(2,1)} %get-tuple-element.758, s32[]{:T(128)S(6)} %select_n.36), kind=kOutput, calls=%fused_computation.49.clone.1 | convolution fusion | flops 1078984704 | bytes 23068932 | tf_op jit(solution)/shard_map/while/body/eval_jaxpr/gij,gik->gjk/dot_general | solution.py:72
  791.6 8.1 copy.39
  799.7 14.1 %convolution_add_fusion.24 = f32[128,32768]{1,0:T(8,128)} fusion(f32[128,32768]{1,0:T(8,128)} %get-tuple-element.741, pred[]{:T(512)S(6)} %compare.11, f32[64,32768]{1,0:T(8,128)S(1)} %bitcast.103, s32[64]{0:T(128)S(1)} %dynamic_slice.111), kind=kOutput, calls=%fused_computation.42.clone.1 | convolution fusion | flops 547364864 | bytes 41943296 | tf_op jit(solution)/shard_map/while/body/eval_jaxpr/dot_general | solution.py:31
  813.8 14.0 %convolution_add_fusion.25 = f32[128,32768]{1,0:T(8,128)} fusion(f32[128,32768]{1,0:T(8,128)} %convolution_add_fusion.24, f32[64,32768]{1,0:T(8,128)S(1)} %bitcast.104, s32[64]{0:T(128)S(1)} %dynamic_slice.111), kind=kOutput, calls=%fused_computation.41.clone.1 | convolution fusion | flops 549462016 | bytes 41943296 | tf_op jit(solution)/shard_map/while/body/eval_jaxpr/dot_general | solution.py:31
  827.8 10.6 %convolution_add_fusion.26 = f32[128,32768]{1,0:T(8,128)} fusion(f32[128,32768]{1,0:T(8,128)} %convolution_add_fusion.25, f32[64,32768]{1,0:T(8,128)S(1)} %bitcast.105, s32[64]{0:T(128)S(1)} %dynamic_slice.111), kind=kOutput, calls=%fused_computation.40.clone.1 | convolution fusion | flops 555753472 | bytes 41943296 | tf_op jit(solution)/shard_map/while/body/eval_jaxpr/dot_general | solution.py:31
  838.4 18.0 %reshape.118 = f32[16384,256]{1,0:T(8,128)} reshape(f32[128,32768]{1,0:T(8,128)} %get-tuple-element.391) | data formatting | bytes 33554432 | tf_op jit(solution)/shard_map/reshape | solution.py:87
  856.4 110.8 %reduce-scatter.2.cloned.1.call-done = f32[1024,256]{1,0:T(8,128)} async-done(((f32[16384,256]{1,0:T(8,128)}), f32[1024,256]{1,0:T(8,128)}) %reduce-scatter.2.cloned.1.call-update) | async-done | bytes 1048592 | tf_op jit(solution)/shard_map/reduce_scatter | solution.py:88
  (144 shorter events, 206.4 us)
Async XLA Ops:
  7.2 76.7 %all-gather.2.cloned.1.call-start = ((), (), s32[]{:S(2)}) async-start(), calls=%async_computation.1 | async-start | bytes 8912896 | tf_op jit(solution)/shard_map/all_gather | solution.py:40
  9.3 316.2 %all-reduce.3.cloned.1.call-start = ((), (), s32[]{:S(2)}) async-start(), calls=%async_computation.2 | async-start | bytes 8388608 | tf_op jit(solution)/shard_map/psum | solution.py:84
  16.0 81.4 %copy-start.3 = (s32[1,1,256]{2,1,0:T(1,128)S(1)}, s32[1,1,256]{2,1,0:T(1,128)}, u32[]{:S(2)}) copy-start(s32[1,1,256]{2,1,0:T(1,128)} %param.16) | copy-start | bytes 3076
  97.4 11.5 %copy-start.5 = (s32[1,1,256]{2,1,0:T(1,128)S(1)}, s32[1,1,256]{2,1,0:T(1,128)}, u32[]{:S(2)}) copy-start(s32[1,1,256]{2,1,0:T(1,128)} %param.15) | copy-start | bytes 3076
  130.5 8.3 copy-start
  165.2 8.3 copy-start
  200.0 8.3 copy-start
  234.8 8.3 copy-start
  253.0 299.3 %all-reduce.5.cloned.1.call-start = ((), (), s32[]{:S(2)}) async-start(), calls=%async_computation.3 | async-start | bytes 8388608 | tf_op jit(solution)/shard_map/psum | solution.py:84
  356.8 8.3 copy-start.1
  391.6 8.3 copy-start.1
  426.3 8.3 copy-start.1
  461.1 8.3 copy-start.1
  479.5 487.7 %reduce-scatter.2.cloned.1.call-start = ((), (), s32[]{:S(2)}) async-start(), calls=%async_computation.4 | async-start | bytes 17825792 | tf_op jit(solution)/shard_map/reduce_scatter | solution.py:88
  562.5 2.4 copy-start.4
  856.4 110.8 %copy-start.2 = (f32[1024,256]{1,0:T(8,128)S(1)}, f32[1024,256]{1,0:T(8,128)}, u32[]{:S(2)}) copy-start(f32[1024,256]{1,0:T(8,128)} %param.13) | copy-start | bytes 3145732
Sparse Core Ops, SparseCore 0:
  10.7 73.1 all-gather.1
  253.1 72.3 all-reduce.2
  479.6 72.6 all-reduce.4
  856.5 110.6 reduce-scatter.1
where the time goes:
time: 982 us; the launch traced here: 976 us
  matrix products  353 us (36%)
  waiting for transfers between devices  312 us (32%)
  local copies, waits for them, and re-layouts  263 us (27%)
  other arithmetic  32.8 us (3%)
  between operations  14 us (1%)
    dot_general x36, matrix products, spread_add(): lax.dot_general(table, piece, dims, preferred_element_type=jnp.float32)  189 us
    while x52, local copies, waits for them, and re-layouts  171 us
    psum x2, waiting for transfers between devices, shards(): grad_x = lax.psum(partial_rows, 'narrow')  133 us
    reduce_scatter x1, waiting for transfers between devices, shards(): lax.psum_scatter(partial_cols, 'wide', scatter_dimension=0, tiled=True)  111 us
    dot_general x8, matrix products, visit(): jnp.einsum('gij,gjk->gik', slope, ys, preferred_element_type=jnp.float32)  86.8 us
    all_gather x1, waiting for transfers between devices, shards(): lax.all_gather(y_cols.astype(jnp.bfloat16), 'wide', axis=0, tiled=True)  67.9 us
    dot_general x4, matrix products, visit(): jnp.einsum('gij,gik->gjk', slope, xs, preferred_element_type=jnp.float32)  43.3 us
    dot_general x13, matrix products, pick_rows(): jnp.dot(table, flat, preferred_element_type=jnp.float32)  33.3 us
  transfers between devices with their start and end apart: 4, of which 4 were waited for; matrix products, arithmetic and copies ran while one was open for 2% of the time, Pallas kernels for 0%

commit v1 on v0

v1 whole, which is shorter than its diff:
```python
import functools

import jax
import jax.numpy as jnp
from jax import lax
from jax.experimental import pallas as pl
from jax.experimental.pallas import tpu as pltpu
from jax.sharding import PartitionSpec as P

huber_delta = 1.0
step_rows = 0.008
penalty = 3.0
step_columns = 0.012

BATCH = 16
LINK = jnp.bfloat16


def shrink(value, level):
    return jnp.sign(value) * jnp.maximum(jnp.abs(value) - level, 0.0)


def sweep_kernel(want_rows, tile, rows_ref, cols_ref, cnt_ref, x_ref, y_ref, v_ref, out_ref, acc_ref):
    step = pl.program_id(0)
    count = cnt_ref[0]

    @pl.when(step == 0)
    def _():
        acc_ref[...] = jnp.zeros_like(acc_ref)

    def body(j, carry):
        s = step * BATCH + j

        @pl.when(s < count)
        def _():
            r = rows_ref[s]
            c = cols_ref[s]
            r0 = pl.multiple_of(r * tile, tile)
            c0 = pl.multiple_of(c * tile, tile)
            xs = x_ref[pl.ds(r0, tile), :]
            ys = y_ref[pl.ds(c0, tile), :]
            pred = lax.dot_general(xs, ys, (((1,), (1,)), ((), ())), preferred_element_type=jnp.float32)
            vals = v_ref[j].astype(jnp.float32)
            slope = jnp.clip(pred - vals, -huber_delta, huber_delta).astype(jnp.bfloat16)
            if want_rows:
                contrib = jnp.dot(slope, ys, preferred_element_type=jnp.float32)
                acc_ref[pl.ds(r0, tile), :] += contrib
            else:
                contrib = lax.dot_general(slope, xs, (((0,), (0,)), ((), ())), preferred_element_type=jnp.float32)
                acc_ref[pl.ds(c0, tile), :] += contrib

        return carry

    lax.fori_loop(0, BATCH, body, 0)

    @pl.when(step == pl.num_programs(0) - 1)
    def _():
        out_ref[...] = acc_ref[...].astype(out_ref.dtype)


def sweep(want_rows, xb, yb, values, rows_index, cols_index, filled):
    slots, tile, _ = values.shape
    segments = xb.shape[0] if want_rows else yb.shape[0]
    rank = xb.shape[1]
    batches = slots // BATCH

    def v_map(i, rows_ref, cols_ref, cnt_ref):
        last = jnp.maximum(cnt_ref[0] - 1, 0) // BATCH
        return (jnp.minimum(i, last), 0, 0)

    grid_spec = pltpu.PrefetchScalarGridSpec(
        num_scalar_prefetch=3,
        grid=(batches,),
        in_specs=[
            pl.BlockSpec(memory_space=pltpu.VMEM),
            pl.BlockSpec(memory_space=pltpu.VMEM),
            pl.BlockSpec((BATCH, tile, tile), v_map),
        ],
        out_specs=pl.BlockSpec((segments, rank), lambda i, *_: (0, 0)),
        scratch_shapes=[pltpu.VMEM((segments, rank), jnp.float32)],
    )
    flops = 4 * slots * tile * tile * rank
    cost = pl.CostEstimate(
        flops=flops,
        transcendentals=0,
        bytes_accessed=values.size * 2 + xb.size * 2 + yb.size * 2 + segments * rank * 2,
    )
    return pl.pallas_call(
        functools.partial(sweep_kernel, want_rows, tile),
        grid_spec=grid_spec,
        out_shape=jax.ShapeDtypeStruct((segments, rank), LINK),
        compiler_params=pltpu.CompilerParams(
            dimension_semantics=("arbitrary",),
            vmem_limit_bytes=60 * 1024 * 1024,
        ),
        cost_estimate=cost,
    )(rows_index, cols_index, filled, xb, yb, values)


def shards(x_rows, y_cols, tile_values, tile_row, tile_col, tile_count):
    slots = tile_row.shape[-1]
    tile = tile_values.shape[-1]
    yb = lax.all_gather(y_cols.astype(jnp.bfloat16), "wide", axis=0, tiled=True)
    values = tile_values.reshape(slots, tile, tile)
    rows_index = tile_row.reshape(slots)
    cols_index = tile_col.reshape(slots)
    filled = tile_count.reshape(1)

    x_now = x_rows
    for turn in range(2):
        xb = x_now.astype(jnp.bfloat16)
        partial_rows = sweep(True, xb, yb, values, rows_index, cols_index, filled)
        grad_x = lax.psum(partial_rows, "narrow").astype(jnp.float32)
        x_now = shrink(x_now - step_rows * grad_x, step_rows * penalty)
    xb = x_now.astype(jnp.bfloat16)
    partial_cols = sweep(False, xb, yb, values, rows_index, cols_index, filled)
    grad_y = lax.psum_scatter(partial_cols, "wide", scatter_dimension=0, tiled=True).astype(jnp.float32)
    return (x_now, y_cols - step_columns * grad_y)


def solution(mesh):
    placed = (
        P("wide", None),
        P(("wide", "narrow"), None),
        P("wide", "narrow", None, None, None),
        P("wide", "narrow", None),
        P("wide", "narrow", None),
        P("wide", "narrow"),
    )
    return jax.shard_map(
        shards,
        mesh=mesh,
        in_specs=placed,
        out_specs=(P("wide", None), P(("wide", "narrow"), None)),
        check_vma=False,
    )
```

time: 982 us -> 600 us (0.61)
  matrix products: 353 us -> 0 us
  local copies, waits for them, and re-layouts: 263 us -> 0.01 us
  Pallas kernels: 0 us -> 135 us
  waiting for transfers between devices: 312 us -> 426 us
    dot_general x61 -> x0, matrix products: 353 us -> none  [the longest x36 189 us: spread_add(): lax.dot_general(table, piece, dims, preferred_element_type=jnp.float32)]
    while x52 -> x0, local copies, waits for them, and re-layouts: 171 us -> none
    pallas_call x0 -> x3, Pallas kernels: none -> 135 us  [sweep(): pl.pallas_call(functools.partial(sweep_kernel, want_rows, tile), grid_spe...]
    psum x2, waiting for transfers between devices: 133 us -> 217 us  [shards(): grad_x = lax.psum(partial_rows, 'narrow').astype(jnp.float32)]
    reshape x4 -> x0, local copies, waits for them, and re-layouts: 41.3 us -> none  [the longest x1 18 us: shards(): partial_cols = sweep(x_blocks, False).reshape(col_blocks * tile, rank)]
    dynamic_slice x28 -> x0, local copies, waits for them, and re-layouts: 30.7 us -> none  [the longest x12 29.5 us: visit(): lax.dynamic_slice_in_dim(y_slots, start, width, 0)]
    reduce_scatter x1, waiting for transfers between devices: 111 us -> 139 us  [shards(): lax.psum_scatter(partial_cols, 'wide', scatter_dimension=0, tiled=True)]
    unnamed x9 -> x4, local copies, waits for them, and re-layouts: 12 us -> 0.01 us
  transfers between devices with their start and end apart: 4 -> 4, of which waited for: 4 -> 4; matrix products, arithmetic and copies ran while one was open for 2% -> 1% of each run, Pallas kernels for 0% -> 0%
where the time goes in v1:
time: 600 us; the launch traced here: 599 us
  waiting for transfers between devices  426 us (71%)
  Pallas kernels  135 us (22%)
  other arithmetic  23.5 us (4%)
  between operations  14.4 us (2%)
    psum x2, waiting for transfers between devices, shards(): grad_x = lax.psum(partial_rows, 'narrow').astype(jnp.float32)  217 us
    reduce_scatter x1, waiting for transfers between devices, shards(): lax.psum_scatter(partial_cols, 'wide', scatter_dimension=0, tiled=True)  139 us
    pallas_call x3, Pallas kernels, sweep(): pl.pallas_call(functools.partial(sweep_kernel, want_rows, tile), grid_spe...  135 us
    all_gather x1, waiting for transfers between devices, shards(): yb = lax.all_gather(y_cols.astype(jnp.bfloat16), 'wide', axis=0, tiled=True)  70.2 us
    convert_element_type x3, other arithmetic, shards(): xb = x_now.astype(jnp.bfloat16)  19.3 us
  transfers between devices with their start and end apart: 4, of which 4 were waited for; matrix products, arithmetic and copies ran while one was open for 1% of the time, Pallas kernels for 0%

profile of v1, /device:TPU:0, one launch (start us, length us, event | category | flops | bytes accessed | tf_op | source)
XLA Modules:
  0.0 598.9 jit_solution(4480656345492680633)
XLA Ops:
  7.2 0.0 all-gather.2.cloned.1.call-start
  7.2 2.1 convert_element_type.22
  9.3 0.0 all-gather.2.cloned.1.call-update
  9.3 0.0 all-reduce.3.cloned.1.call-start
  10.0 3.7 convert_element_type.21.x_ref
  13.7 70.2 %all-gather.2.cloned.1.call-done.y_ref = bf16[16384,256]{1,0:T(8,128)(2,1)} async-done(((bf16[1024,256]{1,0:T(8,128)(2,1)}), bf16[16384,256]{1,0:T(8,128)(2,1)}) %all-gather.2.cloned.1.call-update) | async-done | bytes 8388624 | tf_op jit(solution)/shard_map/all_gather | solution.py:103
  83.9 41.6 %shard_map.77 = bf16[4096,256]{1,0:T(8,128)(2,1)} custom-call(s32[256]{0:T(256)} %bitcast.10, s32[256]{0:T(256)} %bitcast.13, s32[1]{0:T(128)} %bitcast.4.cnt_ref, bf16[4096,256]{1,0:T(8,128)(2,1)} %convert_element_type.21.x_ref, bf16[16384,256]{1,0:T(8,128)(2,1)} %all-gather.2.cloned.1.call-done.y_ref, bf16[256,128,128]{2,1,0:T(8,128)(2,1)} %bitcast.7), custom_call_target="tpu_custom_call" | custom-call | flops 4294967296 | bytes 20971520 | tf_op jit(solution)/shard_map/pallas_call | solution.py:88
  125.5 0.0 all-reduce.3.cloned.1.call-update
  125.5 0.0 all-reduce.5.cloned.1.call-start
  125.5 107.9 %all-reduce.3.cloned.1.call-done = bf16[4096,256]{1,0:T(8,128)(2,1)} async-done(((bf16[4096,256]{1,0:T(8,128)(2,1)}), bf16[4096,256]{1,0:T(8,128)(2,1)}) %all-reduce.3.cloned.1.call-update) | async-done | bytes 2097168 | tf_op jit(solution)/shard_map/psum | solution.py:113
  233.5 6.1 %fusion.x_ref = bf16[4096,256]{1,0:T(8,128)(2,1)} fusion(f32[4096,256]{1,0:T(8,128)} %param.6, bf16[4096,256]{1,0:T(8,128)(2,1)} %all-reduce.3.cloned.1.call-done), kind=kLoop, calls=%fused_computation.2 | loop fusion | flops 9437184 | bytes 8388608 | tf_op jit(solution)/shard_map/convert_element_type | solution.py:111
  239.6 0.0 copy-start
  239.6 41.6 %shard_map.78 = bf16[4096,256]{1,0:T(8,128)(2,1)} custom-call(s32[256]{0:T(256)} %bitcast.11, s32[256]{0:T(256)} %bitcast.14, s32[1]{0:T(128)} %bitcast.5.cnt_ref, bf16[4096,256]{1,0:T(8,128)(2,1)} %fusion.x_ref, bf16[16384,256]{1,0:T(8,128)(2,1)} %all-gather.2.cloned.1.call-done.y_ref, bf16[256,128,128]{2,1,0:T(8,128)(2,1)} %bitcast.8), custom_call_target="tpu_custom_call" | custom-call | flops 4294967296 | bytes 20971520 | tf_op jit(solution)/shard_map/pallas_call | solution.py:88
  281.2 0.0 all-reduce.5.cloned.1.call-update
  281.3 0.0 reduce-scatter.2.cloned.1.call-start
  281.3 108.8 %all-reduce.5.cloned.1.call-done = bf16[4096,256]{1,0:T(8,128)(2,1)} async-done(((bf16[4096,256]{1,0:T(8,128)(2,1)}), bf16[4096,256]{1,0:T(8,128)(2,1)}) %all-reduce.5.cloned.1.call-update) | async-done | bytes 2097168 | tf_op jit(solution)/shard_map/psum | solution.py:113
  390.2 0.0 copy-done
  390.2 9.4 %fusion.1 = (bf16[4096,256]{1,0:T(8,128)(2,1)}, f32[4096,256]{1,0:T(8,128)}) fusion(bf16[4096,256]{1,0:T(8,128)(2,1)} %all-reduce.5.cloned.1.call-done, f32[4096,256]{1,0:T(8,128)} %param.6, bf16[4096,256]{1,0:T(8,128)(2,1)S(1)} %copy-done), kind=kLoop, calls=%fused_computation.4 | loop fusion | flops 17825792 | bytes 14680064 | tf_op jit(solution)/shard_map/convert_element_type | solution.py:115
  399.6 51.9 %shard_map.79 = bf16[16384,256]{1,0:T(8,128)(2,1)} custom-call(s32[256]{0:T(256)} %bitcast.12, s32[256]{0:T(256)} %bitcast.15, s32[1]{0:T(128)} %bitcast.6.cnt_ref, bf16[4096,256]{1,0:T(8,128)(2,1)} %get-tuple-element.2.x_ref, bf16[16384,256]{1,0:T(8,128)(2,1)} %all-gather.2.cloned.1.call-done.y_ref, bf16[256,128,128]{2,1,0:T(8,128)(2,1)} %bitcast.9), custom_call_target="tpu_custom_call" | custom-call | flops 4294967296 | bytes 27262976 | tf_op jit(solution)/shard_map/pallas_call | solution.py:88
  451.5 0.0 copy-start.1
  451.5 0.0 reduce-scatter.2.cloned.1.call-update
  451.5 138.8 %reduce-scatter.2.cloned.1.call-done = bf16[1024,256]{1,0:T(8,128)(2,1)} async-done(((bf16[16384,256]{1,0:T(8,128)(2,1)}), bf16[1024,256]{1,0:T(8,128)(2,1)}) %reduce-scatter.2.cloned.1.call-update) | async-done | bytes 524304 | tf_op jit(solution)/shard_map/reduce_scatter | solution.py:117
  590.3 0.0 copy-done.1
  590.3 2.1 multiply_subtract_fusion
Async XLA Ops:
  7.2 76.7 %all-gather.2.cloned.1.call-start = ((), (), s32[]{:S(2)}) async-start(), calls=%async_computation.1 | async-start | bytes 8912896 | tf_op jit(solution)/shard_map/all_gather | solution.py:103
  9.3 224.1 %all-reduce.3.cloned.1.call-start = ((), (), s32[]{:S(2)}) async-start(), calls=%async_computation.2 | async-start | bytes 4194304 | tf_op jit(solution)/shard_map/psum | solution.py:113
  125.5 264.7 %all-reduce.5.cloned.1.call-start = ((), (), s32[]{:S(2)}) async-start(), calls=%async_computation.3 | async-start | bytes 4194304 | tf_op jit(solution)/shard_map/psum | solution.py:113
  239.6 150.6 %copy-start = (bf16[4096,256]{1,0:T(8,128)(2,1)S(1)}, bf16[4096,256]{1,0:T(8,128)(2,1)}, u32[]{:S(2)}) copy-start(bf16[4096,256]{1,0:T(8,128)(2,1)} %all-reduce.3.cloned.1.call-done) | copy-start | bytes 6291460
  281.3 309.0 %reduce-scatter.2.cloned.1.call-start = ((), (), s32[]{:S(2)}) async-start(), calls=%async_computation.4 | async-start | bytes 8912896 | tf_op jit(solution)/shard_map/reduce_scatter | solution.py:117
  451.5 138.8 %copy-start.1 = (f32[1024,256]{1,0:T(8,128)S(1)}, f32[1024,256]{1,0:T(8,128)}, u32[]{:S(2)}) copy-start(f32[1024,256]{1,0:T(8,128)} %param.7) | copy-start | bytes 3145732
Sparse Core Ops, SparseCore 0:
  10.7 73.1 all-gather.1
  125.6 107.8 all-reduce.2
  281.4 108.7 all-reduce.4
  451.6 138.5 reduce-scatter.1

commit v2 on v1

--- a/solution.py
+++ b/solution.py
@@ -13,7 +13,6 @@
 step_columns = 0.012
 
 BATCH = 16
-LINK = jnp.bfloat16
 
 
 def shrink(value, level):
@@ -28,37 +27,31 @@
     def _():
         acc_ref[...] = jnp.zeros_like(acc_ref)
 
-    def body(j, carry):
-        s = step * BATCH + j
-
-        @pl.when(s < count)
-        def _():
-            r = rows_ref[s]
-            c = cols_ref[s]
-            r0 = pl.multiple_of(r * tile, tile)
-            c0 = pl.multiple_of(c * tile, tile)
+    @pl.when(step * BATCH < count)
+    def _():
+        parts = []
+        for j in range(BATCH):
+            s = step * BATCH + j
+            r0 = pl.multiple_of(rows_ref[s] * tile, tile)
+            c0 = pl.multiple_of(cols_ref[s] * tile, tile)
             xs = x_ref[pl.ds(r0, tile), :]
             ys = y_ref[pl.ds(c0, tile), :]
             pred = lax.dot_general(xs, ys, (((1,), (1,)), ((), ())), preferred_element_type=jnp.float32)
             vals = v_ref[j].astype(jnp.float32)
-            slope = jnp.clip(pred - vals, -huber_delta, huber_delta).astype(jnp.bfloat16)
+            slope = jnp.where(s < count, jnp.clip(pred - vals, -huber_delta, huber_delta), 0.0).astype(jnp.bfloat16)
             if want_rows:
-                contrib = jnp.dot(slope, ys, preferred_element_type=jnp.float32)
-                acc_ref[pl.ds(r0, tile), :] += contrib
+                parts.append((r0, jnp.dot(slope, ys, preferred_element_type=jnp.float32)))
             else:
-                contrib = lax.dot_general(slope, xs, (((0,), (0,)), ((), ())), preferred_element_type=jnp.float32)
-                acc_ref[pl.ds(c0, tile), :] += contrib
-
-        return carry
-
-    lax.fori_loop(0, BATCH, body, 0)
+                parts.append((c0, lax.dot_general(slope, xs, (((0,), (0,)), ((), ())), preferred_element_type=jnp.float32)))
+        for o0, contrib in parts:
+            acc_ref[pl.ds(o0, tile), :] += contrib
 
     @pl.when(step == pl.num_programs(0) - 1)
     def _():
         out_ref[...] = acc_ref[...].astype(out_ref.dtype)
 
 
-def sweep(want_rows, xb, yb, values, rows_index, cols_index, filled):
+def sweep(want_rows, xb, yb, values, rows_index, cols_index, filled, link):
     slots, tile, _ = values.shape
     segments = xb.shape[0] if want_rows else yb.shape[0]
     rank = xb.shape[1]
@@ -88,7 +81,7 @@
     return pl.pallas_call(
         functools.partial(sweep_kernel, want_rows, tile),
         grid_spec=grid_spec,
-        out_shape=jax.ShapeDtypeStruct((segments, rank), LINK),
+        out_shape=jax.ShapeDtypeStruct((segments, rank), link),
         compiler_params=pltpu.CompilerParams(
             dimension_semantics=("arbitrary",),
             vmem_limit_bytes=60 * 1024 * 1024,
@@ -109,11 +102,11 @@
     x_now = x_rows
     for turn in range(2):
         xb = x_now.astype(jnp.bfloat16)
-        partial_rows = sweep(True, xb, yb, values, rows_index, cols_index, filled)
-        grad_x = lax.psum(partial_rows, "narrow").astype(jnp.float32)
+        partial_rows = sweep(True, xb, yb, values, rows_index, cols_index, filled, jnp.float32)
+        grad_x = lax.psum(partial_rows, "narrow")
         x_now = shrink(x_now - step_rows * grad_x, step_rows * penalty)
     xb = x_now.astype(jnp.bfloat16)
-    partial_cols = sweep(False, xb, yb, values, rows_index, cols_index, filled)
+    partial_cols = sweep(False, xb, yb, values, rows_index, cols_index, filled, jnp.bfloat16)
     grad_y = lax.psum_scatter(partial_cols, "wide", scatter_dimension=0, tiled=True).astype(jnp.float32)
     return (x_now, y_cols - step_columns * grad_y)
 

time: 600 us -> 412 us (0.69)
  Pallas kernels: 135 us -> 36.4 us
  waiting for transfers between devices: 426 us -> 335 us
    pallas_call x3, Pallas kernels: 135 us -> 36.4 us  [sweep(): pl.pallas_call(functools.partial(sweep_kernel, want_rows, tile), grid_spe...]
    psum x2, waiting for transfers between devices: 217 us -> 167 us  [shards(): grad_x = lax.psum(partial_rows, 'narrow')]
    reduce_scatter x1, waiting for transfers between devices: 139 us -> 98.3 us  [shards(): lax.psum_scatter(partial_cols, 'wide', scatter_dimension=0, tiled=True)]
where the time goes in v2:
time: 412 us
  waiting for transfers between devices  335 us (81%)
  Pallas kernels  36.4 us (9%)
  other arithmetic  25.6 us (6%)
  between operations  14.4 us (3%)
    psum x2, waiting for transfers between devices, shards(): grad_x = lax.psum(partial_rows, 'narrow')  167 us
    reduce_scatter x1, waiting for transfers between devices, shards(): lax.psum_scatter(partial_cols, 'wide', scatter_dimension=0, tiled=True)  98.3 us
    all_gather x1, waiting for transfers between devices, shards(): yb = lax.all_gather(y_cols.astype(jnp.bfloat16), 'wide', axis=0, tiled=True)  70.1 us
    pallas_call x3, Pallas kernels, sweep(): pl.pallas_call(functools.partial(sweep_kernel, want_rows, tile), grid_spe...  36.4 us
    convert_element_type x3, other arithmetic, shards(): xb = x_now.astype(jnp.bfloat16)  21.4 us
  transfers between devices with their start and end apart: 4, of which 4 were waited for; matrix products, arithmetic and copies ran while one was open for 1% of the time, Pallas kernels for 0%

profile of v2, /device:TPU:0, one launch (start us, length us, event | category | flops | bytes accessed | tf_op | source)
XLA Modules:
  0.0 411.9 jit_solution(6737503612572442618)
XLA Ops:
  7.2 0.0 all-gather.2.cloned.1.call-start
  7.2 2.1 convert_element_type.16
  9.3 0.0 all-gather.2.cloned.1.call-update
  9.3 0.0 all-reduce.3.cloned.1.call-start
  10.0 3.8 convert_element_type.15.x_ref
  13.8 70.1 %all-gather.2.cloned.1.call-done.y_ref = bf16[16384,256]{1,0:T(8,128)(2,1)} async-done(((bf16[1024,256]{1,0:T(8,128)(2,1)}), bf16[16384,256]{1,0:T(8,128)(2,1)}) %all-gather.2.cloned.1.call-update) | async-done | bytes 8388624 | tf_op jit(solution)/shard_map/all_gather | solution.py:96
  83.9 11.2 %shard_map.77 = f32[4096,256]{1,0:T(8,128)} custom-call(s32[256]{0:T(256)} %bitcast.10, s32[256]{0:T(256)} %bitcast.13, s32[1]{0:T(128)} %bitcast.4.cnt_ref, bf16[4096,256]{1,0:T(8,128)(2,1)} %convert_element_type.15.x_ref, bf16[16384,256]{1,0:T(8,128)(2,1)} %all-gather.2.cloned.1.call-done.y_ref, bf16[256,128,128]{2,1,0:T(8,128)(2,1)} %bitcast.7), custom_call_target="tpu_custom_call" | custom-call | flops 4294967296 | bytes 20971520 | tf_op jit(solution)/shard_map/pallas_call | solution.py:81
  95.0 0.0 all-reduce.3.cloned.1.call-update
  95.1 0.0 all-reduce.5.cloned.1.call-start
  95.1 83.4 %all-reduce.3.cloned.1.call-done = f32[4096,256]{1,0:T(8,128)} async-done(((f32[4096,256]{1,0:T(8,128)}), f32[4096,256]{1,0:T(8,128)}) %all-reduce.3.cloned.1.call-update) | async-done | bytes 4194320 | tf_op jit(solution)/shard_map/psum | solution.py:106
  178.5 6.6 %fusion.x_ref = bf16[4096,256]{1,0:T(8,128)(2,1)} fusion(f32[4096,256]{1,0:T(8,128)} %param.6, f32[4096,256]{1,0:T(8,128)} %all-reduce.3.cloned.1.call-done), kind=kLoop, calls=%fused_computation.3 | loop fusion | flops 8388608 | bytes 10485760 | tf_op jit(solution)/shard_map/convert_element_type | solution.py:104
  185.1 11.2 %shard_map.78 = f32[4096,256]{1,0:T(8,128)} custom-call(s32[256]{0:T(256)} %bitcast.11, s32[256]{0:T(256)} %bitcast.14, s32[1]{0:T(128)} %bitcast.5.cnt_ref, bf16[4096,256]{1,0:T(8,128)(2,1)} %fusion.x_ref, bf16[16384,256]{1,0:T(8,128)(2,1)} %all-gather.2.cloned.1.call-done.y_ref, bf16[256,128,128]{2,1,0:T(8,128)(2,1)} %bitcast.8), custom_call_target="tpu_custom_call" | custom-call | flops 4294967296 | bytes 20971520 | tf_op jit(solution)/shard_map/pallas_call | solution.py:81
  196.3 0.0 all-reduce.5.cloned.1.call-update
  196.3 0.2 reduce-scatter.2.cloned.1.call-start
  196.5 83.4 %all-reduce.5.cloned.1.call-done = f32[4096,256]{1,0:T(8,128)} async-done(((f32[4096,256]{1,0:T(8,128)}), f32[4096,256]{1,0:T(8,128)}) %all-reduce.5.cloned.1.call-update) | async-done | bytes 4194320 | tf_op jit(solution)/shard_map/psum | solution.py:106
  279.9 11.0 %fusion.1 = (bf16[4096,256]{1,0:T(8,128)(2,1)}, f32[4096,256]{1,0:T(8,128)}) fusion(f32[4096,256]{1,0:T(8,128)} %all-reduce.5.cloned.1.call-done, f32[4096,256]{1,0:T(8,128)} %param.6, f32[4096,256]{1,0:T(8,128)} %all-reduce.3.cloned.1.call-done), kind=kLoop, calls=%fused_computation.4 | loop fusion | flops 15728640 | bytes 18874368 | tf_op jit(solution)/shard_map/convert_element_type | solution.py:108
  290.9 14.0 %shard_map.79 = bf16[16384,256]{1,0:T(8,128)(2,1)} custom-call(s32[256]{0:T(256)} %bitcast.12, s32[256]{0:T(256)} %bitcast.15, s32[1]{0:T(128)} %bitcast.6.cnt_ref, bf16[4096,256]{1,0:T(8,128)(2,1)} %get-tuple-element.2.x_ref, bf16[16384,256]{1,0:T(8,128)(2,1)} %all-gather.2.cloned.1.call-done.y_ref, bf16[256,128,128]{2,1,0:T(8,128)(2,1)} %bitcast.9), custom_call_target="tpu_custom_call" | custom-call | flops 4294967296 | bytes 27262976 | tf_op jit(solution)/shard_map/pallas_call | solution.py:81
  304.9 0.0 copy-start
  304.9 0.0 reduce-scatter.2.cloned.1.call-update
  304.9 98.3 %reduce-scatter.2.cloned.1.call-done = bf16[1024,256]{1,0:T(8,128)(2,1)} async-done(((bf16[16384,256]{1,0:T(8,128)(2,1)}), bf16[1024,256]{1,0:T(8,128)(2,1)}) %reduce-scatter.2.cloned.1.call-update) | async-done | bytes 524304 | tf_op jit(solution)/shard_map/reduce_scatter | solution.py:110
  403.3 0.0 copy-done
  403.3 2.1 multiply_subtract_fusion
Async XLA Ops:
  7.2 76.7 %all-gather.2.cloned.1.call-start = ((), (), s32[]{:S(2)}) async-start(), calls=%async_computation.1 | async-start | bytes 8912896 | tf_op jit(solution)/shard_map/all_gather | solution.py:96
  9.3 169.2 %all-reduce.3.cloned.1.call-start = ((), (), s32[]{:S(2)}) async-start(), calls=%async_computation.2 | async-start | bytes 8388608 | tf_op jit(solution)/shard_map/psum | solution.py:106
  95.1 184.8 %all-reduce.5.cloned.1.call-start = ((), (), s32[]{:S(2)}) async-start(), calls=%async_computation.3 | async-start | bytes 8388608 | tf_op jit(solution)/shard_map/psum | solution.py:106
  196.3 207.0 %reduce-scatter.2.cloned.1.call-start = ((), (), s32[]{:S(2)}) async-start(), calls=%async_computation.4 | async-start | bytes 8912896 | tf_op jit(solution)/shard_map/reduce_scatter | solution.py:110
  304.9 98.4 %copy-start = (f32[1024,256]{1,0:T(8,128)S(1)}, f32[1024,256]{1,0:T(8,128)}, u32[]{:S(2)}) copy-start(f32[1024,256]{1,0:T(8,128)} %param.7) | copy-start | bytes 3145732
Sparse Core Ops, SparseCore 0:
  10.7 73.1 all-gather.1
  95.2 83.2 all-reduce.2
  196.4 83.4 all-reduce.4
  305.0 98.1 reduce-scatter.1

commit v3 on v2

--- a/solution.py
+++ b/solution.py
@@ -34,7 +34,7 @@
             s = step * BATCH + j
             r0 = pl.multiple_of(rows_ref[s] * tile, tile)
             c0 = pl.multiple_of(cols_ref[s] * tile, tile)
-            xs = x_ref[pl.ds(r0, tile), :]
+            xs = x_ref[pl.ds(r0, tile), :].astype(jnp.bfloat16)
             ys = y_ref[pl.ds(c0, tile), :]
             pred = lax.dot_general(xs, ys, (((1,), (1,)), ((), ())), preferred_element_type=jnp.float32)
             vals = v_ref[j].astype(jnp.float32)
@@ -76,7 +76,7 @@
     cost = pl.CostEstimate(
         flops=flops,
         transcendentals=0,
-        bytes_accessed=values.size * 2 + xb.size * 2 + yb.size * 2 + segments * rank * 2,
+        bytes_accessed=values.size * 2 + xb.size * xb.dtype.itemsize + yb.size * 2 + segments * rank * 2,
     )
     return pl.pallas_call(
         functools.partial(sweep_kernel, want_rows, tile),
@@ -99,14 +99,21 @@
     cols_index = tile_col.reshape(slots)
     filled = tile_count.reshape(1)
 
-    x_now = x_rows
-    for turn in range(2):
-        xb = x_now.astype(jnp.bfloat16)
-        partial_rows = sweep(True, xb, yb, values, rows_index, cols_index, filled, jnp.float32)
-        grad_x = lax.psum(partial_rows, "narrow")
-        x_now = shrink(x_now - step_rows * grad_x, step_rows * penalty)
-    xb = x_now.astype(jnp.bfloat16)
-    partial_cols = sweep(False, xb, yb, values, rows_index, cols_index, filled, jnp.bfloat16)
+    rows_here = x_rows.shape[0] // lax.axis_size("narrow")
+    first = lax.axis_index("narrow") * rows_here
+    level = step_rows * penalty
+
+    partial_rows = sweep(True, x_rows.astype(jnp.bfloat16), yb, values, rows_index, cols_index, filled, jnp.float32)
+    grad_x = lax.psum_scatter(partial_rows, "narrow", scatter_dimension=0, tiled=True)
+    x_mine = shrink(lax.dynamic_slice_in_dim(x_rows, first, rows_here, 0) - step_rows * grad_x, level)
+    xb = lax.all_gather(x_mine.astype(jnp.bfloat16), "narrow", axis=0, tiled=True)
+
+    partial_rows = sweep(True, xb, yb, values, rows_index, cols_index, filled, jnp.float32)
+    grad_x = lax.psum_scatter(partial_rows, "narrow", scatter_dimension=0, tiled=True)
+    x_mine = shrink(x_mine - step_rows * grad_x, level)
+    x_now = lax.all_gather(x_mine, "narrow", axis=0, tiled=True)
+
+    partial_cols = sweep(False, x_now, yb, values, rows_index, cols_index, filled, jnp.bfloat16)
     grad_y = lax.psum_scatter(partial_cols, "wide", scatter_dimension=0, tiled=True).astype(jnp.float32)
     return (x_now, y_cols - step_columns * grad_y)
 

time: 412 us -> 396 us (0.961)
  waiting for transfers between devices: 335 us -> 305 us
  Pallas kernels: 36.4 us -> 57.7 us
  other arithmetic: 25.6 us -> 12.5 us
  local copies, waits for them, and re-layouts: 0.01 us -> 4.48 us
    psum x2 -> x0, waiting for transfers between devices: 167 us -> none  [shards(): grad_x = lax.psum(partial_rows, 'narrow')]
    reduce_scatter x0 -> x2, waiting for transfers between devices: none -> 87.4 us  [shards(): lax.psum_scatter(partial_rows, 'narrow', scatter_dimension=0, tiled=True)]
    all_gather x0 -> x2, waiting for transfers between devices: none -> 55.4 us  [the longest x1 31.1 us: shards(): x_now = lax.all_gather(x_mine, 'narrow', axis=0, tiled=True)]
    pallas_call x3, Pallas kernels: 36.4 us -> 57.7 us  [sweep(): pl.pallas_call(functools.partial(sweep_kernel, want_rows, tile), grid_spe...]
    convert_element_type x3 -> x2, other arithmetic: 21.4 us -> 5.9 us  [the longest x1 3.76 us: shards(): x_rows.astype(jnp.bfloat16)]
    reduce_scatter x1, waiting for transfers between devices: 98.3 us -> 91.9 us  [shards(): lax.psum_scatter(partial_cols, 'wide', scatter_dimension=0, tiled=True)]
    unnamed x2 -> x5, local copies, waits for them, and re-layouts: 0.01 us -> 4.48 us
  transfers between devices with their start and end apart: 4 -> 6, of which waited for: 4 -> 6; matrix products, arithmetic and copies ran while one was open for 1% -> 1% of each run, Pallas kernels for 0% -> 0%
where the time goes in v3:
time: 396 us; the launch traced here: 395 us
  waiting for transfers between devices  305 us (77%)
  Pallas kernels  57.7 us (15%)
  between operations  14.8 us (4%)
  other arithmetic  12.5 us (3%)
  local copies, waits for them, and re-layouts  4.48 us (1%)
    reduce_scatter x1, waiting for transfers between devices, shards(): lax.psum_scatter(partial_cols, 'wide', scatter_dimension=0, tiled=True)  91.9 us
    reduce_scatter x2, waiting for transfers between devices, shards(): lax.psum_scatter(partial_rows, 'narrow', scatter_dimension=0, tiled=True)  87.4 us
    all_gather x1, waiting for transfers between devices, shards(): yb = lax.all_gather(y_cols.astype(jnp.bfloat16), 'wide', axis=0, tiled=True)  70.1 us
    pallas_call x3, Pallas kernels, sweep(): pl.pallas_call(functools.partial(sweep_kernel, want_rows, tile), grid_spe...  57.7 us
    all_gather x1, waiting for transfers between devices, shards(): x_now = lax.all_gather(x_mine, 'narrow', axis=0, tiled=True)  31.1 us
    all_gather x1, waiting for transfers between devices, shards(): lax.all_gather(x_mine.astype(jnp.bfloat16), 'narrow', axis=0, tiled=True)  24.3 us
  transfers between devices with their start and end apart: 6, of which 6 were waited for; matrix products, arithmetic and copies ran while one was open for 1% of the time, Pallas kernels for 0%

profile of v3, /device:TPU:0, one launch (start us, length us, event | category | flops | bytes accessed | tf_op | source)
XLA Modules:
  0.0 394.7 jit_solution(2075659002595451020)
XLA Ops:
  7.2 0.0 all-gather.4.cloned.1.call-start
  7.2 2.1 convert_element_type.13
  9.3 0.0 all-gather.4.cloned.1.call-update
  9.3 0.0 reduce-scatter.4.cloned.1.call-start
  10.0 3.8 convert_element_type.12.x_ref
  13.8 70.1 %all-gather.4.cloned.1.call-done.y_ref = bf16[16384,256]{1,0:T(8,128)(2,1)} async-done(((bf16[1024,256]{1,0:T(8,128)(2,1)}), bf16[16384,256]{1,0:T(8,128)(2,1)}) %all-gather.4.cloned.1.call-update) | async-done | bytes 8388624 | tf_op jit(solution)/shard_map/all_gather | solution.py:96
  83.9 17.8 %shard_map.77 = f32[4096,256]{1,0:T(8,128)} custom-call(s32[256]{0:T(256)} %bitcast.10, s32[256]{0:T(256)} %bitcast.13, s32[1]{0:T(128)} %bitcast.4.cnt_ref, bf16[4096,256]{1,0:T(8,128)(2,1)} %convert_element_type.12.x_ref, bf16[16384,256]{1,0:T(8,128)(2,1)} %all-gather.4.cloned.1.call-done.y_ref, bf16[256,128,128]{2,1,0:T(8,128)(2,1)} %bitcast.7), custom_call_target="tpu_custom_call" | custom-call | flops 4294967296 | bytes 20971520 | tf_op jit(solution)/shard_map/pallas_call | solution.py:81
  101.7 0.0 reduce-scatter.4.cloned.1.call-update
  101.7 0.0 all-gather.6.cloned.1.call-start
  101.8 43.5 %reduce-scatter.4.cloned.1.call-done = f32[512,256]{1,0:T(8,128)} async-done(((f32[4096,256]{1,0:T(8,128)}), f32[512,256]{1,0:T(8,128)}) %reduce-scatter.4.cloned.1.call-update) | async-done | bytes 524304 | tf_op jit(solution)/shard_map/reduce_scatter | solution.py:107
  145.2 2.1 fusion
  147.4 0.0 all-gather.6.cloned.1.call-update
  147.4 0.0 reduce-scatter.6.cloned.1.call-start
  147.5 24.3 %all-gather.6.cloned.1.call-done.x_ref = bf16[4096,256]{1,0:T(8,128)(2,1)} async-done(((bf16[512,256]{1,0:T(8,128)(2,1)}), bf16[4096,256]{1,0:T(8,128)(2,1)}) %all-gather.6.cloned.1.call-update) | async-done | bytes 2097168 | tf_op jit(solution)/shard_map/all_gather | solution.py:109
  171.8 17.8 %shard_map.78 = f32[4096,256]{1,0:T(8,128)} custom-call(s32[256]{0:T(256)} %bitcast.11, s32[256]{0:T(256)} %bitcast.14, s32[1]{0:T(128)} %bitcast.5.cnt_ref, bf16[4096,256]{1,0:T(8,128)(2,1)} %all-gather.6.cloned.1.call-done.x_ref, bf16[16384,256]{1,0:T(8,128)(2,1)} %all-gather.4.cloned.1.call-done.y_ref, bf16[256,128,128]{2,1,0:T(8,128)(2,1)} %bitcast.8), custom_call_target="tpu_custom_call" | custom-call | flops 4294967296 | bytes 20971520 | tf_op jit(solution)/shard_map/pallas_call | solution.py:81
  189.6 0.0 copy-start.1
  189.6 0.0 reduce-scatter.6.cloned.1.call-update
  189.6 0.0 all-gather.8.cloned.1.call-start
  189.7 44.0 %reduce-scatter.6.cloned.1.call-done = f32[512,256]{1,0:T(8,128)} async-done(((f32[4096,256]{1,0:T(8,128)}), f32[512,256]{1,0:T(8,128)}) %reduce-scatter.6.cloned.1.call-update) | async-done | bytes 524304 | tf_op jit(solution)/shard_map/reduce_scatter | solution.py:112
  233.6 0.0 copy-done.1
  233.6 2.4 maximum_multiply_fusion
  236.1 0.0 all-gather.8.cloned.1.call-update
  236.1 0.0 reduce-scatter.8.cloned.1.call-start
  236.2 31.1 %all-gather.8.cloned.1.call-done.x_ref = f32[4096,256]{1,0:T(8,128)} async-done(((f32[512,256]{1,0:T(8,128)}), f32[4096,256]{1,0:T(8,128)}) %all-gather.8.cloned.1.call-update) | async-done | bytes 4194320 | tf_op jit(solution)/shard_map/all_gather | solution.py:114
  267.3 22.0 %shard_map.79 = bf16[16384,256]{1,0:T(8,128)(2,1)} custom-call(s32[256]{0:T(256)} %bitcast.12, s32[256]{0:T(256)} %bitcast.15, s32[1]{0:T(128)} %bitcast.6.cnt_ref, f32[4096,256]{1,0:T(8,128)} %all-gather.8.cloned.1.call-done.x_ref, bf16[16384,256]{1,0:T(8,128)(2,1)} %all-gather.4.cloned.1.call-done.y_ref, bf16[256,128,128]{2,1,0:T(8,128)(2,1)} %bitcast.9), custom_call_target="tpu_custom_call" | custom-call | flops 4294967296 | bytes 29360128 | tf_op jit(solution)/shard_map/pallas_call | solution.py:81
  289.3 0.0 copy-start
  289.3 0.0 reduce-scatter.8.cloned.1.call-update
  289.3 91.9 %reduce-scatter.8.cloned.1.call-done = bf16[1024,256]{1,0:T(8,128)(2,1)} async-done(((bf16[16384,256]{1,0:T(8,128)(2,1)}), bf16[1024,256]{1,0:T(8,128)(2,1)}) %reduce-scatter.8.cloned.1.call-update) | async-done | bytes 524304 | tf_op jit(solution)/shard_map/reduce_scatter | solution.py:117
  381.2 0.0 copy-done
  381.2 2.1 multiply_subtract_fusion
  383.3 4.5 %copy.10 = f32[4096,256]{1,0:T(8,128)} copy(f32[4096,256]{1,0:T(8,128)} %all-gather.8.cloned.1.call-done.x_ref) | data formatting | bytes 8388608
Async XLA Ops:
  7.2 76.7 %all-gather.4.cloned.1.call-start = ((), (), s32[]{:S(2)}) async-start(), calls=%async_computation.3 | async-start | bytes 8912896 | tf_op jit(solution)/shard_map/all_gather | solution.py:96
  9.3 135.9 %reduce-scatter.4.cloned.1.call-start = ((), (), s32[]{:S(2)}) async-start(), calls=%async_computation.4 | async-start | bytes 4718592 | tf_op jit(solution)/shard_map/reduce_scatter | solution.py:107
  101.7 70.0 %all-gather.6.cloned.1.call-start = ((), (), s32[]{:S(2)}) async-start(), calls=%async_computation.5 | async-start | bytes 2359296 | tf_op jit(solution)/shard_map/all_gather | solution.py:109
  147.4 86.2 %reduce-scatter.6.cloned.1.call-start = ((), (), s32[]{:S(2)}) async-start(), calls=%async_computation.6 | async-start | bytes 4718592 | tf_op jit(solution)/shard_map/reduce_scatter | solution.py:112
  189.6 44.0 %copy-start.1 = (f32[512,256]{1,0:T(8,128)S(1)}, f32[512,256]{1,0:T(8,128)}, u32[]{:S(2)}) copy-start(f32[512,256]{1,0:T(8,128)} %reduce-scatter.4.cloned.1.call-done) | copy-start | bytes 1572868
  189.6 77.6 %all-gather.8.cloned.1.call-start = ((), (), s32[]{:S(2)}) async-start(), calls=%async_computation.7 | async-start | bytes 4718592 | tf_op jit(solution)/shard_map/all_gather | solution.py:114
  236.1 145.1 %reduce-scatter.8.cloned.1.call-start = ((), (), s32[]{:S(2)}) async-start(), calls=%async_computation.8 | async-start | bytes 8912896 | tf_op jit(solution)/shard_map/reduce_scatter | solution.py:117
  289.3 91.9 %copy-start = (f32[1024,256]{1,0:T(8,128)S(1)}, f32[1024,256]{1,0:T(8,128)}, u32[]{:S(2)}) copy-start(f32[1024,256]{1,0:T(8,128)} %param.7) | copy-start | bytes 3145732
Sparse Core Ops, SparseCore 0:
  10.7 73.1 all-gather.3
  101.9 43.3 reduce-scatter.3
  147.5 24.1 all-gather.5
  189.7 43.8 reduce-scatter.5
  236.2 31.0 all-gather.7
  289.4 91.7 reduce-scatter.7

commit v4 on v3

--- a/solution.py
+++ b/solution.py
@@ -12,20 +12,23 @@
 penalty = 3.0
 step_columns = 0.012
 
-BATCH = 16
+BATCH = 32
 
 
 def shrink(value, level):
     return jnp.sign(value) * jnp.maximum(jnp.abs(value) - level, 0.0)
 
 
-def sweep_kernel(want_rows, tile, rows_ref, cols_ref, cnt_ref, x_ref, y_ref, v_ref, out_ref, acc_ref):
+def sweep_kernel(want_rows, tile, rows_ref, cols_ref, cnt_ref, x_ref, y_ref, v_ref, out_ref, *rest):
+    acc_ref = rest[-1]
     step = pl.program_id(0)
     count = cnt_ref[0]
 
     @pl.when(step == 0)
     def _():
         acc_ref[...] = jnp.zeros_like(acc_ref)
+        if len(rest) > 1:
+            rest[0][...] = x_ref[...]
 
     @pl.when(step * BATCH < count)
     def _():
@@ -51,7 +54,7 @@
         out_ref[...] = acc_ref[...].astype(out_ref.dtype)
 
 
-def sweep(want_rows, xb, yb, values, rows_index, cols_index, filled, link):
+def sweep(want_rows, xb, yb, values, rows_index, cols_index, filled, link, echo=False):
     slots, tile, _ = values.shape
     segments = xb.shape[0] if want_rows else yb.shape[0]
     rank = xb.shape[1]
@@ -69,7 +72,8 @@
             pl.BlockSpec(memory_space=pltpu.VMEM),
             pl.BlockSpec((BATCH, tile, tile), v_map),
         ],
-        out_specs=pl.BlockSpec((segments, rank), lambda i, *_: (0, 0)),
+        out_specs=[pl.BlockSpec((segments, rank), lambda i, *_: (0, 0))]
+        + ([pl.BlockSpec(xb.shape, lambda i, *_: (0, 0))] if echo else []),
         scratch_shapes=[pltpu.VMEM((segments, rank), jnp.float32)],
     )
     flops = 4 * slots * tile * tile * rank
@@ -78,16 +82,18 @@
         transcendentals=0,
         bytes_accessed=values.size * 2 + xb.size * xb.dtype.itemsize + yb.size * 2 + segments * rank * 2,
     )
-    return pl.pallas_call(
+    outs = pl.pallas_call(
         functools.partial(sweep_kernel, want_rows, tile),
         grid_spec=grid_spec,
-        out_shape=jax.ShapeDtypeStruct((segments, rank), link),
+        out_shape=[jax.ShapeDtypeStruct((segments, rank), link)]
+        + ([jax.ShapeDtypeStruct(xb.shape, xb.dtype)] if echo else []),
         compiler_params=pltpu.CompilerParams(
             dimension_semantics=("arbitrary",),
             vmem_limit_bytes=60 * 1024 * 1024,
         ),
         cost_estimate=cost,
     )(rows_index, cols_index, filled, xb, yb, values)
+    return outs if echo else outs[0]
 
 
 def shards(x_rows, y_cols, tile_values, tile_row, tile_col, tile_count):
@@ -113,9 +119,9 @@
     x_mine = shrink(x_mine - step_rows * grad_x, level)
     x_now = lax.all_gather(x_mine, "narrow", axis=0, tiled=True)
 
-    partial_cols = sweep(False, x_now, yb, values, rows_index, cols_index, filled, jnp.bfloat16)
+    partial_cols, x_out = sweep(False, x_now, yb, values, rows_index, cols_index, filled, jnp.bfloat16, echo=True)
     grad_y = lax.psum_scatter(partial_cols, "wide", scatter_dimension=0, tiled=True).astype(jnp.float32)
-    return (x_now, y_cols - step_columns * grad_y)
+    return (x_out, y_cols - step_columns * grad_y)
 
 
 def solution(mesh):

time: 396 us -> 380 us (0.960)
  Pallas kernels: 57.7 us -> 51.9 us
  waiting for transfers between devices: 305 us -> 300 us
  local copies, waits for them, and re-layouts: 4.48 us -> 0.01 us
    pallas_call x3, Pallas kernels: 57.7 us -> 51.9 us  [sweep(): pl.pallas_call(functools.partial(sweep_kernel, want_rows, tile), grid_spe...]
    unnamed x5 -> x4, local copies, waits for them, and re-layouts: 4.48 us -> 0.01 us
where the time goes in v4:
time: 380 us; the launch traced here: 379 us
  waiting for transfers between devices  300 us (79%)
  Pallas kernels  51.9 us (14%)
  between operations  14.8 us (4%)
  other arithmetic  12.5 us (3%)
    reduce_scatter x1, waiting for transfers between devices, shards(): lax.psum_scatter(partial_cols, 'wide', scatter_dimension=0, tiled=True)  90 us
    reduce_scatter x2, waiting for transfers between devices, shards(): lax.psum_scatter(partial_rows, 'narrow', scatter_dimension=0, tiled=True)  84.3 us
    all_gather x1, waiting for transfers between devices, shards(): yb = lax.all_gather(y_cols.astype(jnp.bfloat16), 'wide', axis=0, tiled=True)  70.1 us
    pallas_call x3, Pallas kernels, sweep(): pl.pallas_call(functools.partial(sweep_kernel, want_rows, tile), grid_spe...  51.9 us
    all_gather x1, waiting for transfers between devices, shards(): x_now = lax.all_gather(x_mine, 'narrow', axis=0, tiled=True)  31 us
    all_gather x1, waiting for transfers between devices, shards(): lax.all_gather(x_mine.astype(jnp.bfloat16), 'narrow', axis=0, tiled=True)  24.4 us
  transfers between devices with their start and end apart: 6, of which 6 were waited for; matrix products, arithmetic and copies ran while one was open for 1% of the time, Pallas kernels for 0%

profile of v4, /device:TPU:0, one launch (start us, length us, event | category | flops | bytes accessed | tf_op | source)
XLA Modules:
  0.0 379.4 jit_solution(410176379001363306)
XLA Ops:
  7.2 0.0 all-gather.4.cloned.1.call-start
  7.2 2.1 convert_element_type.13
  9.3 0.0 all-gather.4.cloned.1.call-update
  9.3 0.0 reduce-scatter.4.cloned.1.call-start
  10.0 3.8 convert_element_type.12.x_ref
  13.8 70.1 %all-gather.4.cloned.1.call-done.y_ref = bf16[16384,256]{1,0:T(8,128)(2,1)} async-done(((bf16[1024,256]{1,0:T(8,128)(2,1)}), bf16[16384,256]{1,0:T(8,128)(2,1)}) %all-gather.4.cloned.1.call-update) | async-done | bytes 8388624 | tf_op jit(solution)/shard_map/all_gather | solution.py:102
  83.9 15.4 %shard_map.77 = f32[4096,256]{1,0:T(8,128)} custom-call(s32[256]{0:T(256)} %bitcast.10, s32[256]{0:T(256)} %bitcast.13, s32[1]{0:T(128)} %bitcast.4.cnt_ref, bf16[4096,256]{1,0:T(8,128)(2,1)} %convert_element_type.12.x_ref, bf16[16384,256]{1,0:T(8,128)(2,1)} %all-gather.4.cloned.1.call-done.y_ref, bf16[256,128,128]{2,1,0:T(8,128)(2,1)} %bitcast.7), custom_call_target="tpu_custom_call" | custom-call | flops 4294967296 | bytes 20971520 | tf_op jit(solution)/shard_map/pallas_call | solution.py:85
  99.3 0.0 reduce-scatter.4.cloned.1.call-update
  99.3 0.0 all-gather.6.cloned.1.call-start
  99.4 41.9 %reduce-scatter.4.cloned.1.call-done = f32[512,256]{1,0:T(8,128)} async-done(((f32[4096,256]{1,0:T(8,128)}), f32[512,256]{1,0:T(8,128)}) %reduce-scatter.4.cloned.1.call-update) | async-done | bytes 524304 | tf_op jit(solution)/shard_map/reduce_scatter | solution.py:113
  141.3 2.1 fusion
  143.4 0.0 all-gather.6.cloned.1.call-update
  143.5 0.0 reduce-scatter.6.cloned.1.call-start
  143.5 24.4 %all-gather.6.cloned.1.call-done.x_ref = bf16[4096,256]{1,0:T(8,128)(2,1)} async-done(((bf16[512,256]{1,0:T(8,128)(2,1)}), bf16[4096,256]{1,0:T(8,128)(2,1)}) %all-gather.6.cloned.1.call-update) | async-done | bytes 2097168 | tf_op jit(solution)/shard_map/all_gather | solution.py:115
  167.9 15.4 %shard_map.78 = f32[4096,256]{1,0:T(8,128)} custom-call(s32[256]{0:T(256)} %bitcast.11, s32[256]{0:T(256)} %bitcast.14, s32[1]{0:T(128)} %bitcast.5.cnt_ref, bf16[4096,256]{1,0:T(8,128)(2,1)} %all-gather.6.cloned.1.call-done.x_ref, bf16[16384,256]{1,0:T(8,128)(2,1)} %all-gather.4.cloned.1.call-done.y_ref, bf16[256,128,128]{2,1,0:T(8,128)(2,1)} %bitcast.8), custom_call_target="tpu_custom_call" | custom-call | flops 4294967296 | bytes 20971520 | tf_op jit(solution)/shard_map/pallas_call | solution.py:85
  183.3 0.0 copy-start.1
  183.3 0.0 reduce-scatter.6.cloned.1.call-update
  183.3 0.0 all-gather.8.cloned.1.call-start
  183.4 42.4 %reduce-scatter.6.cloned.1.call-done = f32[512,256]{1,0:T(8,128)} async-done(((f32[4096,256]{1,0:T(8,128)}), f32[512,256]{1,0:T(8,128)}) %reduce-scatter.6.cloned.1.call-update) | async-done | bytes 524304 | tf_op jit(solution)/shard_map/reduce_scatter | solution.py:118
  225.8 0.0 copy-done.1
  225.8 2.4 maximum_multiply_fusion
  228.2 0.0 all-gather.8.cloned.1.call-update
  228.3 0.0 reduce-scatter.8.cloned.1.call-start
  228.3 31.0 %all-gather.8.cloned.1.call-done.x_ref = f32[4096,256]{1,0:T(8,128)} async-done(((f32[512,256]{1,0:T(8,128)}), f32[4096,256]{1,0:T(8,128)}) %all-gather.8.cloned.1.call-update) | async-done | bytes 4194320 | tf_op jit(solution)/shard_map/all_gather | solution.py:120
  259.3 21.0 %shard_map.79 = (bf16[16384,256]{1,0:T(8,128)(2,1)}, f32[4096,256]{1,0:T(8,128)}) custom-call(s32[256]{0:T(256)} %bitcast.12, s32[256]{0:T(256)} %bitcast.15, s32[1]{0:T(128)} %bitcast.6.cnt_ref, f32[4096,256]{1,0:T(8,128)} %all-gather.8.cloned.1.call-done.x_ref, bf16[16384,256]{1,0:T(8,128)(2,1)} %all-gather.4.cloned.1.call-done.y_ref, ...), custom_call_target="tpu_custom_call" | custom-call | flops 4294967296 | bytes 29360128 | tf_op jit(solution)/shard_map/pallas_call | solution.py:85
  280.4 0.0 copy-start
  280.4 0.0 reduce-scatter.8.cloned.1.call-update
  280.4 90.0 %reduce-scatter.8.cloned.1.call-done = bf16[1024,256]{1,0:T(8,128)(2,1)} async-done(((bf16[16384,256]{1,0:T(8,128)(2,1)}), bf16[1024,256]{1,0:T(8,128)(2,1)}) %reduce-scatter.8.cloned.1.call-update) | async-done | bytes 524304 | tf_op jit(solution)/shard_map/reduce_scatter | solution.py:123
  370.4 0.0 copy-done
  370.4 2.1 multiply_subtract_fusion
Async XLA Ops:
  7.2 76.7 %all-gather.4.cloned.1.call-start = ((), (), s32[]{:S(2)}) async-start(), calls=%async_computation.3 | async-start | bytes 8912896 | tf_op jit(solution)/shard_map/all_gather | solution.py:102
  9.3 132.0 %reduce-scatter.4.cloned.1.call-start = ((), (), s32[]{:S(2)}) async-start(), calls=%async_computation.4 | async-start | bytes 4718592 | tf_op jit(solution)/shard_map/reduce_scatter | solution.py:113
  99.3 68.6 %all-gather.6.cloned.1.call-start = ((), (), s32[]{:S(2)}) async-start(), calls=%async_computation.5 | async-start | bytes 2359296 | tf_op jit(solution)/shard_map/all_gather | solution.py:115
  143.5 82.3 %reduce-scatter.6.cloned.1.call-start = ((), (), s32[]{:S(2)}) async-start(), calls=%async_computation.6 | async-start | bytes 4718592 | tf_op jit(solution)/shard_map/reduce_scatter | solution.py:118
  183.3 42.5 %copy-start.1 = (f32[512,256]{1,0:T(8,128)S(1)}, f32[512,256]{1,0:T(8,128)}, u32[]{:S(2)}) copy-start(f32[512,256]{1,0:T(8,128)} %reduce-scatter.4.cloned.1.call-done) | copy-start | bytes 1572868
  183.3 76.0 %all-gather.8.cloned.1.call-start = ((), (), s32[]{:S(2)}) async-start(), calls=%async_computation.7 | async-start | bytes 4718592 | tf_op jit(solution)/shard_map/all_gather | solution.py:120
  228.3 142.1 %reduce-scatter.8.cloned.1.call-start = ((), (), s32[]{:S(2)}) async-start(), calls=%async_computation.8 | async-start | bytes 8912896 | tf_op jit(solution)/shard_map/reduce_scatter | solution.py:123
  280.4 90.0 %copy-start = (f32[1024,256]{1,0:T(8,128)S(1)}, f32[1024,256]{1,0:T(8,128)}, u32[]{:S(2)}) copy-start(f32[1024,256]{1,0:T(8,128)} %param.7) | copy-start | bytes 3145732
Sparse Core Ops, SparseCore 0:
  10.7 73.1 all-gather.3
  99.4 41.8 reduce-scatter.3
  143.6 24.2 all-gather.5
  183.5 42.2 reduce-scatter.5
  228.4 30.9 all-gather.7
  280.5 89.8 reduce-scatter.7

commit v5 on v3

--- a/solution.py
+++ b/solution.py
@@ -12,7 +12,7 @@
 penalty = 3.0
 step_columns = 0.012
 
-BATCH = 16
+BATCH = 64
 
 
 def shrink(value, level):
@@ -36,13 +36,15 @@
             c0 = pl.multiple_of(cols_ref[s] * tile, tile)
             xs = x_ref[pl.ds(r0, tile), :].astype(jnp.bfloat16)
             ys = y_ref[pl.ds(c0, tile), :]
-            pred = lax.dot_general(xs, ys, (((1,), (1,)), ((), ())), preferred_element_type=jnp.float32)
             vals = v_ref[j].astype(jnp.float32)
-            slope = jnp.where(s < count, jnp.clip(pred - vals, -huber_delta, huber_delta), 0.0).astype(jnp.bfloat16)
             if want_rows:
+                pred = lax.dot_general(xs, ys, (((1,), (1,)), ((), ())), preferred_element_type=jnp.float32)
+                slope = jnp.where(s < count, jnp.clip(pred - vals, -huber_delta, huber_delta), 0.0).astype(jnp.bfloat16)
                 parts.append((r0, jnp.dot(slope, ys, preferred_element_type=jnp.float32)))
             else:
-                parts.append((c0, lax.dot_general(slope, xs, (((0,), (0,)), ((), ())), preferred_element_type=jnp.float32)))
+                pred_t = lax.dot_general(ys, xs, (((1,), (1,)), ((), ())), preferred_element_type=jnp.float32)
+                slope_t = jnp.where(s < count, jnp.clip(pred_t - vals, -huber_delta, huber_delta), 0.0).astype(jnp.bfloat16)
+                parts.append((c0, jnp.dot(slope_t, xs, preferred_element_type=jnp.float32)))
         for o0, contrib in parts:
             acc_ref[pl.ds(o0, tile), :] += contrib
 
@@ -111,11 +113,16 @@
     partial_rows = sweep(True, xb, yb, values, rows_index, cols_index, filled, jnp.float32)
     grad_x = lax.psum_scatter(partial_rows, "narrow", scatter_dimension=0, tiled=True)
     x_mine = shrink(x_mine - step_rows * grad_x, level)
-    x_now = lax.all_gather(x_mine, "narrow", axis=0, tiled=True)
+    upper = x_mine.astype(jnp.bfloat16)
+    lower = (x_mine - upper.astype(jnp.float32)).astype(jnp.bfloat16)
+    xb = lax.all_gather(upper, "narrow", axis=0, tiled=True)
+    lower_all = lax.all_gather(lower, "narrow", axis=0, tiled=True)
 
-    partial_cols = sweep(False, x_now, yb, values, rows_index, cols_index, filled, jnp.bfloat16)
+    values_t = jnp.swapaxes(values, 1, 2)
+    partial_cols = sweep(False, xb, yb, values_t, rows_index, cols_index, filled, jnp.bfloat16)
     grad_y = lax.psum_scatter(partial_cols, "wide", scatter_dimension=0, tiled=True).astype(jnp.float32)
-    return (x_now, y_cols - step_columns * grad_y)
+    x_out = xb.astype(jnp.float32) + lower_all.astype(jnp.float32)
+    return (x_out, y_cols - step_columns * grad_y)
 
 
 def solution(mesh):

time: 396 us -> 377 us (0.952)
  waiting for transfers between devices: 305 us -> 275 us
  local copies, waits for them, and re-layouts: 4.48 us -> 12 us
    all_gather x1 -> x2, waiting for transfers between devices: 31.1 us -> 18.4 us  [the longest x1 11.5 us: shards(): xb = lax.all_gather(upper, 'narrow', axis=0, tiled=True)]
    reduce_scatter x2, waiting for transfers between devices: 87.4 us -> 76 us  [shards(): lax.psum_scatter(partial_rows, 'narrow', scatter_dimension=0, tiled=True)]
    unnamed x5, local copies, waits for them, and re-layouts: 4.48 us -> 12 us
    reduce_scatter x1, waiting for transfers between devices: 91.9 us -> 85.4 us  [shards(): lax.psum_scatter(partial_cols, 'wide', scatter_dimension=0, tiled=True)]
    add x0 -> x1, other arithmetic: none -> 4.01 us  [shards(): x_out = xb.astype(jnp.float32) + lower_all.astype(jnp.float32)]
  transfers between devices with their start and end apart: 6 -> 7, of which waited for: 6 -> 7; matrix products, arithmetic and copies ran while one was open for 1% -> 5% of each run, Pallas kernels for 0% -> 6%
where the time goes in v5:
time: 377 us; the launch traced here: 376 us
  waiting for transfers between devices  275 us (73%)
  Pallas kernels  57.8 us (15%)
  other arithmetic  16.2 us (4%)
  between operations  14.8 us (4%)
  local copies, waits for them, and re-layouts  12 us (3%)
    reduce_scatter x1, waiting for transfers between devices, shards(): lax.psum_scatter(partial_cols, 'wide', scatter_dimension=0, tiled=True)  85.4 us
    reduce_scatter x2, waiting for transfers between devices, shards(): lax.psum_scatter(partial_rows, 'narrow', scatter_dimension=0, tiled=True)  76 us
    all_gather x1, waiting for transfers between devices, shards(): yb = lax.all_gather(y_cols.astype(jnp.bfloat16), 'wide', axis=0, tiled=True)  70.1 us
    pallas_call x3, Pallas kernels, sweep(): pl.pallas_call(functools.partial(sweep_kernel, want_rows, tile), grid_spe...  57.8 us
    all_gather x1, waiting for transfers between devices, shards(): lax.all_gather(x_mine.astype(jnp.bfloat16), 'narrow', axis=0, tiled=True)  24.4 us
    unnamed x5, local copies, waits for them, and re-layouts  12 us
    all_gather x1, waiting for transfers between devices, shards(): xb = lax.all_gather(upper, 'narrow', axis=0, tiled=True)  11.5 us
  transfers between devices with their start and end apart: 7, of which 7 were waited for; matrix products, arithmetic and copies ran while one was open for 5% of the time, Pallas kernels for 6%

profile of v5, /device:TPU:0, one launch (start us, length us, event | category | flops | bytes accessed | tf_op | source)
XLA Modules:
  0.0 376.2 jit_solution(6926577188753292967)
XLA Ops:
  7.2 0.0 all-gather.5.cloned.1.call-start
  7.2 2.1 convert_element_type.28
  9.3 0.0 all-gather.5.cloned.1.call-update
  9.3 0.0 reduce-scatter.4.cloned.1.call-start
  10.0 3.8 convert_element_type.27.x_ref
  13.8 70.1 %all-gather.5.cloned.1.call-done.y_ref = bf16[16384,256]{1,0:T(8,128)(2,1)} async-done(((bf16[1024,256]{1,0:T(8,128)(2,1)}), bf16[16384,256]{1,0:T(8,128)(2,1)}) %all-gather.5.cloned.1.call-update) | async-done | bytes 8388624 | tf_op jit(solution)/shard_map/all_gather | solution.py:98
  83.9 18.4 %shard_map.77 = f32[4096,256]{1,0:T(8,128)} custom-call(s32[256]{0:T(256)} %bitcast.13, s32[256]{0:T(256)} %bitcast.16, s32[1]{0:T(128)} %bitcast.7.cnt_ref, bf16[4096,256]{1,0:T(8,128)(2,1)} %convert_element_type.27.x_ref, bf16[16384,256]{1,0:T(8,128)(2,1)} %all-gather.5.cloned.1.call-done.y_ref, bf16[256,128,128]{2,1,0:T(8,128)(2,1)} %bitcast.10), custom_call_target="tpu_custom_call" | custom-call | flops 4294967296 | bytes 20971520 | tf_op jit(solution)/shard_map/pallas_call | solution.py:83
  102.3 0.0 reduce-scatter.4.cloned.1.call-update
  102.3 0.0 all-gather.7.cloned.1.call-start
  102.3 37.7 %reduce-scatter.4.cloned.1.call-done = f32[512,256]{1,0:T(8,128)} async-done(((f32[4096,256]{1,0:T(8,128)}), f32[512,256]{1,0:T(8,128)}) %reduce-scatter.4.cloned.1.call-update) | async-done | bytes 524304 | tf_op jit(solution)/shard_map/reduce_scatter | solution.py:109
  140.1 2.1 fusion.1
  142.2 0.0 all-gather.7.cloned.1.call-update
  142.2 0.0 reduce-scatter.6.cloned.1.call-start
  142.3 24.4 %all-gather.7.cloned.1.call-done.x_ref = bf16[4096,256]{1,0:T(8,128)(2,1)} async-done(((bf16[512,256]{1,0:T(8,128)(2,1)}), bf16[4096,256]{1,0:T(8,128)(2,1)}) %all-gather.7.cloned.1.call-update) | async-done | bytes 2097168 | tf_op jit(solution)/shard_map/all_gather | solution.py:111
  166.7 18.4 %shard_map.78 = f32[4096,256]{1,0:T(8,128)} custom-call(s32[256]{0:T(256)} %bitcast.14, s32[256]{0:T(256)} %bitcast.17, s32[1]{0:T(128)} %bitcast.8.cnt_ref, bf16[4096,256]{1,0:T(8,128)(2,1)} %all-gather.7.cloned.1.call-done.x_ref, bf16[16384,256]{1,0:T(8,128)(2,1)} %all-gather.5.cloned.1.call-done.y_ref, bf16[256,128,128]{2,1,0:T(8,128)(2,1)} %bitcast.11), custom_call_target="tpu_custom_call" | custom-call | flops 4294967296 | bytes 20971520 | tf_op jit(solution)/shard_map/pallas_call | solution.py:83
  185.0 0.0 reduce-scatter.6.cloned.1.call-update
  185.1 0.0 all-gather.9.cloned.1.call-start
  185.1 38.2 %reduce-scatter.6.cloned.1.call-done = f32[512,256]{1,0:T(8,128)} async-done(((f32[4096,256]{1,0:T(8,128)}), f32[512,256]{1,0:T(8,128)}) %reduce-scatter.6.cloned.1.call-update) | async-done | bytes 524304 | tf_op jit(solution)/shard_map/reduce_scatter | solution.py:114
  223.4 2.1 fusion
  225.5 0.0 all-gather.9.cloned.1.call-update
  225.5 0.0 all-gather.11.cloned.1.call-start
  225.5 0.5 all-gather.11.cloned.1.call-update
  226.1 0.2 reduce-scatter.8.cloned.1.call-start
  226.3 12.0 %copy.8 = bf16[1,1,256,128,128]{3,4,2,1,0:T(8,128)(2,1)} copy(bf16[1,1,256,128,128]{4,3,2,1,0:T(8,128)(2,1)} %param.8) | data formatting | bytes 16777216 | tf_op args[2]
  238.3 11.5 %all-gather.9.cloned.1.call-done.x_ref = bf16[4096,256]{1,0:T(8,128)(2,1)} async-done(((bf16[512,256]{1,0:T(8,128)(2,1)}), bf16[4096,256]{1,0:T(8,128)(2,1)}) %all-gather.9.cloned.1.call-update) | async-done | bytes 2097168 | tf_op jit(solution)/shard_map/all_gather | solution.py:118
  249.8 21.0 %shard_map.79 = bf16[16384,256]{1,0:T(8,128)(2,1)} custom-call(s32[256]{0:T(256)} %bitcast.15, s32[256]{0:T(256)} %bitcast.18, s32[1]{0:T(128)} %bitcast.9.cnt_ref, bf16[4096,256]{1,0:T(8,128)(2,1)} %all-gather.9.cloned.1.call-done.x_ref, bf16[16384,256]{1,0:T(8,128)(2,1)} %all-gather.5.cloned.1.call-done.y_ref, bf16[256,128,128]{2,1,0:T(8,128)(2,1)} %bitcast.12), custom_call_target="tpu_custom_call" | custom-call | flops 4294967296 | bytes 27262976 | tf_op jit(solution)/shard_map/pallas_call | solution.py:83
  270.8 0.0 copy-start
  270.8 0.0 reduce-scatter.8.cloned.1.call-update
  270.8 0.0 copy-start.1
  270.8 6.9 %all-gather.11.cloned.1.call-done = bf16[4096,256]{1,0:T(8,128)(2,1)} async-done(((bf16[512,256]{1,0:T(8,128)(2,1)}), bf16[4096,256]{1,0:T(8,128)(2,1)}) %all-gather.11.cloned.1.call-update) | async-done | bytes 2097168 | tf_op jit(solution)/shard_map/all_gather | solution.py:119
  277.8 0.0 copy-done
  277.8 4.0 %convert_add_fusion = f32[4096,256]{1,0:T(8,128)} fusion(bf16[4096,256]{1,0:T(8,128)(2,1)} %all-gather.11.cloned.1.call-done, bf16[4096,256]{1,0:T(8,128)(2,1)S(1)} %copy-done), kind=kLoop, calls=%fused_computation | loop fusion | flops 3145728 | bytes 8388608 | tf_op jit(solution)/shard_map/add | solution.py:124
  281.8 85.4 %reduce-scatter.8.cloned.1.call-done = bf16[1024,256]{1,0:T(8,128)(2,1)} async-done(((bf16[16384,256]{1,0:T(8,128)(2,1)}), bf16[1024,256]{1,0:T(8,128)(2,1)}) %reduce-scatter.8.cloned.1.call-update) | async-done | bytes 524304 | tf_op jit(solution)/shard_map/reduce_scatter | solution.py:123
  367.2 0.0 copy-done.1
  367.2 2.1 multiply_subtract_fusion
Async XLA Ops:
  7.2 76.7 %all-gather.5.cloned.1.call-start = ((), (), s32[]{:S(2)}) async-start(), calls=%async_computation.3 | async-start | bytes 8912896 | tf_op jit(solution)/shard_map/all_gather | solution.py:98
  9.3 130.8 %reduce-scatter.4.cloned.1.call-start = ((), (), s32[]{:S(2)}) async-start(), calls=%async_computation.4 | async-start | bytes 4718592 | tf_op jit(solution)/shard_map/reduce_scatter | solution.py:109
  102.3 64.4 %all-gather.7.cloned.1.call-start = ((), (), s32[]{:S(2)}) async-start(), calls=%async_computation.5 | async-start | bytes 2359296 | tf_op jit(solution)/shard_map/all_gather | solution.py:111
  142.2 81.2 %reduce-scatter.6.cloned.1.call-start = ((), (), s32[]{:S(2)}) async-start(), calls=%async_computation.6 | async-start | bytes 4718592 | tf_op jit(solution)/shard_map/reduce_scatter | solution.py:114
  185.1 64.8 %all-gather.9.cloned.1.call-start = ((), (), s32[]{:S(2)}) async-start(), calls=%async_computation.7 | async-start | bytes 2359296 | tf_op jit(solution)/shard_map/all_gather | solution.py:118
  225.5 52.3 %all-gather.11.cloned.1.call-start = ((), (), s32[]{:S(2)}) async-start(), calls=%async_computation.8 | async-start | bytes 2359296 | tf_op jit(solution)/shard_map/all_gather | solution.py:119
  226.1 141.2 %reduce-scatter.8.cloned.1.call-start = ((), (), s32[]{:S(2)}) async-start(), calls=%async_computation.9 | async-start | bytes 8912896 | tf_op jit(solution)/shard_map/reduce_scatter | solution.py:123
  270.8 7.0 %copy-start = (bf16[4096,256]{1,0:T(8,128)(2,1)S(1)}, bf16[4096,256]{1,0:T(8,128)(2,1)}, u32[]{:S(2)}) copy-start(bf16[4096,256]{1,0:T(8,128)(2,1)} %all-gather.9.cloned.1.call-done.x_ref) | copy-start | bytes 6291460
  270.8 96.4 %copy-start.1 = (f32[1024,256]{1,0:T(8,128)S(1)}, f32[1024,256]{1,0:T(8,128)}, u32[]{:S(2)}) copy-start(f32[1024,256]{1,0:T(8,128)} %param.7) | copy-start | bytes 3145732
Sparse Core Ops, SparseCore 0:
  10.7 73.1 all-gather.4
  102.4 37.6 reduce-scatter.3
  142.4 24.2 all-gather.6
  185.2 38.1 reduce-scatter.5
  225.6 24.1 all-gather.8
  252.0 25.7 all-gather.10
  281.2 86.0 reduce-scatter.7

commit v6 on v4

--- a/solution.py
+++ b/solution.py
@@ -12,23 +12,26 @@
 penalty = 3.0
 step_columns = 0.012
 
-BATCH = 32
+BATCH = 64
 
 
 def shrink(value, level):
     return jnp.sign(value) * jnp.maximum(jnp.abs(value) - level, 0.0)
 
 
-def sweep_kernel(want_rows, tile, rows_ref, cols_ref, cnt_ref, x_ref, y_ref, v_ref, out_ref, *rest):
-    acc_ref = rest[-1]
+def sweep_kernel(want_rows, echo, tile, rows_ref, cols_ref, cnt_ref, x_ref, y_ref, v_ref, *rest):
+    if echo:
+        out_ref, echo_ref, acc_ref = rest
+    else:
+        out_ref, acc_ref = rest[-2:]
     step = pl.program_id(0)
     count = cnt_ref[0]
 
     @pl.when(step == 0)
     def _():
         acc_ref[...] = jnp.zeros_like(acc_ref)
-        if len(rest) > 1:
-            rest[0][...] = x_ref[...]
+        if echo:
+            echo_ref[...] = x_ref[...]
 
     @pl.when(step * BATCH < count)
     def _():
@@ -39,13 +42,15 @@
             c0 = pl.multiple_of(cols_ref[s] * tile, tile)
             xs = x_ref[pl.ds(r0, tile), :].astype(jnp.bfloat16)
             ys = y_ref[pl.ds(c0, tile), :]
-            pred = lax.dot_general(xs, ys, (((1,), (1,)), ((), ())), preferred_element_type=jnp.float32)
             vals = v_ref[j].astype(jnp.float32)
-            slope = jnp.where(s < count, jnp.clip(pred - vals, -huber_delta, huber_delta), 0.0).astype(jnp.bfloat16)
             if want_rows:
+                pred = lax.dot_general(xs, ys, (((1,), (1,)), ((), ())), preferred_element_type=jnp.float32)
+                slope = jnp.where(s < count, jnp.clip(pred - vals, -huber_delta, huber_delta), 0.0).astype(jnp.bfloat16)
                 parts.append((r0, jnp.dot(slope, ys, preferred_element_type=jnp.float32)))
             else:
-                parts.append((c0, lax.dot_general(slope, xs, (((0,), (0,)), ((), ())), preferred_element_type=jnp.float32)))
+                pred_t = lax.dot_general(ys, xs, (((1,), (1,)), ((), ())), preferred_element_type=jnp.float32)
+                slope_t = jnp.where(s < count, jnp.clip(pred_t - vals, -huber_delta, huber_delta), 0.0).astype(jnp.bfloat16)
+                parts.append((c0, jnp.dot(slope_t, xs, preferred_element_type=jnp.float32)))
         for o0, contrib in parts:
             acc_ref[pl.ds(o0, tile), :] += contrib
 
@@ -54,7 +59,7 @@
         out_ref[...] = acc_ref[...].astype(out_ref.dtype)
 
 
-def sweep(want_rows, xb, yb, values, rows_index, cols_index, filled, link, echo=False):
+def sweep(want_rows, xb, yb, values, rows_index, cols_index, filled, link, echo=False, hold=None):
     slots, tile, _ = values.shape
     segments = xb.shape[0] if want_rows else yb.shape[0]
     rank = xb.shape[1]
@@ -71,7 +76,8 @@
             pl.BlockSpec(memory_space=pltpu.VMEM),
             pl.BlockSpec(memory_space=pltpu.VMEM),
             pl.BlockSpec((BATCH, tile, tile), v_map),
-        ],
+        ]
+        + ([pl.BlockSpec(memory_space=pl.ANY)] if hold is not None else []),
         out_specs=[pl.BlockSpec((segments, rank), lambda i, *_: (0, 0))]
         + ([pl.BlockSpec(xb.shape, lambda i, *_: (0, 0))] if echo else []),
         scratch_shapes=[pltpu.VMEM((segments, rank), jnp.float32)],
@@ -83,7 +89,7 @@
         bytes_accessed=values.size * 2 + xb.size * xb.dtype.itemsize + yb.size * 2 + segments * rank * 2,
     )
     outs = pl.pallas_call(
-        functools.partial(sweep_kernel, want_rows, tile),
+        functools.partial(sweep_kernel, want_rows, echo, tile),
         grid_spec=grid_spec,
         out_shape=[jax.ShapeDtypeStruct((segments, rank), link)]
         + ([jax.ShapeDtypeStruct(xb.shape, xb.dtype)] if echo else []),
@@ -92,7 +98,7 @@
             vmem_limit_bytes=60 * 1024 * 1024,
         ),
         cost_estimate=cost,
-    )(rows_index, cols_index, filled, xb, yb, values)
+    )(rows_index, cols_index, filled, xb, yb, values, *([] if hold is None else [hold]))
     return outs if echo else outs[0]
 
 
@@ -109,7 +115,8 @@
     first = lax.axis_index("narrow") * rows_here
     level = step_rows * penalty
 
-    partial_rows = sweep(True, x_rows.astype(jnp.bfloat16), yb, values, rows_index, cols_index, filled, jnp.float32)
+    values_t = jnp.swapaxes(values, 1, 2)
+    partial_rows = sweep(True, x_rows.astype(jnp.bfloat16), yb, values, rows_index, cols_index, filled, jnp.float32, hold=values_t)
     grad_x = lax.psum_scatter(partial_rows, "narrow", scatter_dimension=0, tiled=True)
     x_mine = shrink(lax.dynamic_slice_in_dim(x_rows, first, rows_here, 0) - step_rows * grad_x, level)
     xb = lax.all_gather(x_mine.astype(jnp.bfloat16), "narrow", axis=0, tiled=True)
@@ -119,7 +126,7 @@
     x_mine = shrink(x_mine - step_rows * grad_x, level)
     x_now = lax.all_gather(x_mine, "narrow", axis=0, tiled=True)
 
-    partial_cols, x_out = sweep(False, x_now, yb, values, rows_index, cols_index, filled, jnp.bfloat16, echo=True)
+    partial_cols, x_out = sweep(False, x_now, yb, values_t, rows_index, cols_index, filled, jnp.bfloat16, echo=True)
     grad_y = lax.psum_scatter(partial_cols, "wide", scatter_dimension=0, tiled=True).astype(jnp.float32)
     return (x_out, y_cols - step_columns * grad_y)
 

time: 380 us -> 375 us (0.987)
  waiting for transfers between devices: 300 us -> 275 us
  local copies, waits for them, and re-layouts: 0.01 us -> 11.9 us
  Pallas kernels: 51.9 us -> 60.1 us
    unnamed x4 -> x5, local copies, waits for them, and re-layouts: 0.01 us -> 11.9 us
    all_gather x1, waiting for transfers between devices: 70.1 us -> 58.2 us  [shards(): yb = lax.all_gather(y_cols.astype(jnp.bfloat16), 'wide', axis=0, tiled=True)]
    reduce_scatter x2, waiting for transfers between devices: 84.3 us -> 75.5 us  [shards(): lax.psum_scatter(partial_rows, 'narrow', scatter_dimension=0, tiled=True)]
    pallas_call x3, Pallas kernels: 51.9 us -> 60.1 us  [sweep(): pl.pallas_call(functools.partial(sweep_kernel, want_rows, echo, tile), gr...]
    reduce_scatter x1, waiting for transfers between devices: 90 us -> 85.5 us  [shards(): lax.psum_scatter(partial_cols, 'wide', scatter_dimension=0, tiled=True)]
  transfers between devices with their start and end apart: 6 -> 6, of which waited for: 6 -> 6; matrix products, arithmetic and copies ran while one was open for 1% -> 4% of each run, Pallas kernels for 0% -> 0%
where the time goes in v6:
time: 375 us; the launch traced here: 374 us
  waiting for transfers between devices  275 us (73%)
  Pallas kernels  60.1 us (16%)
  between operations  14.8 us (4%)
  other arithmetic  12.5 us (3%)
  local copies, waits for them, and re-layouts  11.9 us (3%)
    reduce_scatter x1, waiting for transfers between devices, shards(): lax.psum_scatter(partial_cols, 'wide', scatter_dimension=0, tiled=True)  85.5 us
    reduce_scatter x2, waiting for transfers between devices, shards(): lax.psum_scatter(partial_rows, 'narrow', scatter_dimension=0, tiled=True)  75.5 us
    pallas_call x3, Pallas kernels, sweep(): pl.pallas_call(functools.partial(sweep_kernel, want_rows, echo, tile), gr...  60.1 us
    all_gather x1, waiting for transfers between devices, shards(): yb = lax.all_gather(y_cols.astype(jnp.bfloat16), 'wide', axis=0, tiled=True)  58.2 us
    all_gather x1, waiting for transfers between devices, shards(): x_now = lax.all_gather(x_mine, 'narrow', axis=0, tiled=True)  31 us
    all_gather x1, waiting for transfers between devices, shards(): lax.all_gather(x_mine.astype(jnp.bfloat16), 'narrow', axis=0, tiled=True)  24.3 us
    unnamed x5, local copies, waits for them, and re-layouts  11.9 us
  transfers between devices with their start and end apart: 6, of which 6 were waited for; matrix products, arithmetic and copies ran while one was open for 4% of the time, Pallas kernels for 0%

profile of v6, /device:TPU:0, one launch (start us, length us, event | category | flops | bytes accessed | tf_op | source)
XLA Modules:
  0.0 374.4 jit_solution(1920310710119177745)
XLA Ops:
  7.2 0.0 all-gather.4.cloned.1.call-start
  7.2 2.1 convert_element_type.13
  9.3 0.0 all-gather.4.cloned.1.call-update
  9.3 0.0 reduce-scatter.4.cloned.1.call-start
  10.0 3.7 convert_element_type.12.x_ref
  13.7 11.9 %copy.8 = bf16[1,1,256,128,128]{3,4,2,1,0:T(8,128)(2,1)} copy(bf16[1,1,256,128,128]{4,3,2,1,0:T(8,128)(2,1)} %param.8) | data formatting | bytes 16777216 | tf_op args[2]
  25.6 58.2 %all-gather.4.cloned.1.call-done.y_ref = bf16[16384,256]{1,0:T(8,128)(2,1)} async-done(((bf16[1024,256]{1,0:T(8,128)(2,1)}), bf16[16384,256]{1,0:T(8,128)(2,1)}) %all-gather.4.cloned.1.call-update) | async-done | bytes 8388624 | tf_op jit(solution)/shard_map/all_gather | solution.py:108
  83.9 18.4 %shard_map.77 = f32[4096,256]{1,0:T(8,128)} custom-call(s32[256]{0:T(256)} %bitcast.14, s32[256]{0:T(256)} %bitcast.17, s32[1]{0:T(128)} %bitcast.7.cnt_ref, bf16[4096,256]{1,0:T(8,128)(2,1)} %convert_element_type.12.x_ref, bf16[16384,256]{1,0:T(8,128)(2,1)} %all-gather.4.cloned.1.call-done.y_ref, bf16[256,128,128]{2,1,0:T(8,128)(2,1)} %bitcast.12, ...), custom_call_target="tpu_custom_call" | custom-call | flops 4294967296 | bytes 20971520 | tf_op jit(solution)/shard_map/pallas_call | solution.py:91
  102.3 0.0 reduce-scatter.4.cloned.1.call-update
  102.3 0.0 all-gather.6.cloned.1.call-start
  102.3 37.5 %reduce-scatter.4.cloned.1.call-done = f32[512,256]{1,0:T(8,128)} async-done(((f32[4096,256]{1,0:T(8,128)}), f32[512,256]{1,0:T(8,128)}) %reduce-scatter.4.cloned.1.call-update) | async-done | bytes 524304 | tf_op jit(solution)/shard_map/reduce_scatter | solution.py:120
  139.9 2.1 fusion
  142.0 0.0 all-gather.6.cloned.1.call-update
  142.0 0.0 reduce-scatter.6.cloned.1.call-start
  142.1 24.3 %all-gather.6.cloned.1.call-done.x_ref = bf16[4096,256]{1,0:T(8,128)(2,1)} async-done(((bf16[512,256]{1,0:T(8,128)(2,1)}), bf16[4096,256]{1,0:T(8,128)(2,1)}) %all-gather.6.cloned.1.call-update) | async-done | bytes 2097168 | tf_op jit(solution)/shard_map/all_gather | solution.py:122
  166.4 18.4 %shard_map.78 = f32[4096,256]{1,0:T(8,128)} custom-call(s32[256]{0:T(256)} %bitcast.15, s32[256]{0:T(256)} %bitcast.18, s32[1]{0:T(128)} %bitcast.8.cnt_ref, bf16[4096,256]{1,0:T(8,128)(2,1)} %all-gather.6.cloned.1.call-done.x_ref, bf16[16384,256]{1,0:T(8,128)(2,1)} %all-gather.4.cloned.1.call-done.y_ref, bf16[256,128,128]{2,1,0:T(8,128)(2,1)} %bitcast.13), custom_call_target="tpu_custom_call" | custom-call | flops 4294967296 | bytes 20971520 | tf_op jit(solution)/shard_map/pallas_call | solution.py:91
  184.8 0.0 copy-start.1
  184.8 0.0 reduce-scatter.6.cloned.1.call-update
  184.8 0.0 all-gather.8.cloned.1.call-start
  184.9 38.0 %reduce-scatter.6.cloned.1.call-done = f32[512,256]{1,0:T(8,128)} async-done(((f32[4096,256]{1,0:T(8,128)}), f32[512,256]{1,0:T(8,128)}) %reduce-scatter.6.cloned.1.call-update) | async-done | bytes 524304 | tf_op jit(solution)/shard_map/reduce_scatter | solution.py:125
  222.9 0.0 copy-done.1
  222.9 2.4 maximum_multiply_fusion
  225.3 0.0 all-gather.8.cloned.1.call-update
  225.3 0.2 reduce-scatter.8.cloned.1.call-start
  225.6 31.0 %all-gather.8.cloned.1.call-done.x_ref = f32[4096,256]{1,0:T(8,128)} async-done(((f32[512,256]{1,0:T(8,128)}), f32[4096,256]{1,0:T(8,128)}) %all-gather.8.cloned.1.call-update) | async-done | bytes 4194320 | tf_op jit(solution)/shard_map/all_gather | solution.py:127
  256.6 23.3 %shard_map.79 = (bf16[16384,256]{1,0:T(8,128)(2,1)}, f32[4096,256]{1,0:T(8,128)}) custom-call(s32[256]{0:T(256)} %bitcast.16, s32[256]{0:T(256)} %bitcast.19, s32[1]{0:T(128)} %bitcast.9.cnt_ref, f32[4096,256]{1,0:T(8,128)} %all-gather.8.cloned.1.call-done.x_ref, bf16[16384,256]{1,0:T(8,128)(2,1)} %all-gather.4.cloned.1.call-done.y_ref, ...), custom_call_target="tpu_custom_call" | custom-call | flops 4294967296 | bytes 29360128 | tf_op jit(solution)/shard_map/pallas_call | solution.py:91
  279.9 0.0 copy-start
  279.9 0.0 reduce-scatter.8.cloned.1.call-update
  280.0 85.5 %reduce-scatter.8.cloned.1.call-done = bf16[1024,256]{1,0:T(8,128)(2,1)} async-done(((bf16[16384,256]{1,0:T(8,128)(2,1)}), bf16[1024,256]{1,0:T(8,128)(2,1)}) %reduce-scatter.8.cloned.1.call-update) | async-done | bytes 524304 | tf_op jit(solution)/shard_map/reduce_scatter | solution.py:130
  365.4 0.0 copy-done
  365.4 2.1 multiply_subtract_fusion
Async XLA Ops:
  7.2 76.7 %all-gather.4.cloned.1.call-start = ((), (), s32[]{:S(2)}) async-start(), calls=%async_computation.3 | async-start | bytes 8912896 | tf_op jit(solution)/shard_map/all_gather | solution.py:108
  9.3 130.6 %reduce-scatter.4.cloned.1.call-start = ((), (), s32[]{:S(2)}) async-start(), calls=%async_computation.4 | async-start | bytes 4718592 | tf_op jit(solution)/shard_map/reduce_scatter | solution.py:120
  102.3 64.1 %all-gather.6.cloned.1.call-start = ((), (), s32[]{:S(2)}) async-start(), calls=%async_computation.5 | async-start | bytes 2359296 | tf_op jit(solution)/shard_map/all_gather | solution.py:122
  142.0 80.9 %reduce-scatter.6.cloned.1.call-start = ((), (), s32[]{:S(2)}) async-start(), calls=%async_computation.6 | async-start | bytes 4718592 | tf_op jit(solution)/shard_map/reduce_scatter | solution.py:125
  184.8 38.1 %copy-start.1 = (f32[512,256]{1,0:T(8,128)S(1)}, f32[512,256]{1,0:T(8,128)}, u32[]{:S(2)}) copy-start(f32[512,256]{1,0:T(8,128)} %reduce-scatter.4.cloned.1.call-done) | copy-start | bytes 1572868
  184.8 71.8 %all-gather.8.cloned.1.call-start = ((), (), s32[]{:S(2)}) async-start(), calls=%async_computation.7 | async-start | bytes 4718592 | tf_op jit(solution)/shard_map/all_gather | solution.py:127
  225.3 140.1 %reduce-scatter.8.cloned.1.call-start = ((), (), s32[]{:S(2)}) async-start(), calls=%async_computation.8 | async-start | bytes 8912896 | tf_op jit(solution)/shard_map/reduce_scatter | solution.py:130
  279.9 85.5 %copy-start = (f32[1024,256]{1,0:T(8,128)S(1)}, f32[1024,256]{1,0:T(8,128)}, u32[]{:S(2)}) copy-start(f32[1024,256]{1,0:T(8,128)} %param.7) | copy-start | bytes 3145732
Sparse Core Ops, SparseCore 0:
  10.7 73.1 all-gather.3
  102.4 37.4 reduce-scatter.3
  142.2 24.1 all-gather.5
  184.9 37.9 reduce-scatter.5
  225.5 31.0 all-gather.7
  280.1 85.2 reduce-scatter.7

commit v7 on v6

--- a/solution.py
+++ b/solution.py
@@ -21,9 +21,10 @@
 
 def sweep_kernel(want_rows, echo, tile, rows_ref, cols_ref, cnt_ref, x_ref, y_ref, v_ref, *rest):
     if echo:
-        out_ref, echo_ref, acc_ref = rest
+        out_ref, echo_ref, acc_ref, xbuf = rest
     else:
         out_ref, acc_ref = rest[-2:]
+        xbuf = x_ref
     step = pl.program_id(0)
     count = cnt_ref[0]
 
@@ -32,6 +33,7 @@
         acc_ref[...] = jnp.zeros_like(acc_ref)
         if echo:
             echo_ref[...] = x_ref[...]
+            xbuf[...] = x_ref[...].astype(jnp.bfloat16)
 
     @pl.when(step * BATCH < count)
     def _():
@@ -40,7 +42,7 @@
             s = step * BATCH + j
             r0 = pl.multiple_of(rows_ref[s] * tile, tile)
             c0 = pl.multiple_of(cols_ref[s] * tile, tile)
-            xs = x_ref[pl.ds(r0, tile), :].astype(jnp.bfloat16)
+            xs = xbuf[pl.ds(r0, tile), :]
             ys = y_ref[pl.ds(c0, tile), :]
             vals = v_ref[j].astype(jnp.float32)
             if want_rows:
@@ -80,7 +82,8 @@
         + ([pl.BlockSpec(memory_space=pl.ANY)] if hold is not None else []),
         out_specs=[pl.BlockSpec((segments, rank), lambda i, *_: (0, 0))]
         + ([pl.BlockSpec(xb.shape, lambda i, *_: (0, 0))] if echo else []),
-        scratch_shapes=[pltpu.VMEM((segments, rank), jnp.float32)],
+        scratch_shapes=[pltpu.VMEM((segments, rank), jnp.float32)]
+        + ([pltpu.VMEM(xb.shape, jnp.bfloat16)] if echo else []),
     )
     flops = 4 * slots * tile * tile * rank
     cost = pl.CostEstimate(
@@ -95,7 +98,7 @@
         + ([jax.ShapeDtypeStruct(xb.shape, xb.dtype)] if echo else []),
         compiler_params=pltpu.CompilerParams(
             dimension_semantics=("arbitrary",),
-            vmem_limit_bytes=60 * 1024 * 1024,
+            vmem_limit_bytes=64000000,
         ),
         cost_estimate=cost,
     )(rows_index, cols_index, filled, xb, yb, values, *([] if hold is None else [hold]))

time: 375 us -> 376 us (level)
  Pallas kernels: 60.1 us -> 44.9 us
  waiting for transfers between devices: 275 us -> 290 us
    pallas_call x3, Pallas kernels: 60.1 us -> 44.9 us  [sweep(): pl.pallas_call(functools.partial(sweep_kernel, want_rows, echo, tile), gr...]
    reduce_scatter x2, waiting for transfers between devices: 75.5 us -> 86.1 us  [shards(): lax.psum_scatter(partial_rows, 'narrow', scatter_dimension=0, tiled=True)]
    reduce_scatter x1, waiting for transfers between devices: 85.5 us -> 90.4 us  [shards(): lax.psum_scatter(partial_cols, 'wide', scatter_dimension=0, tiled=True)]
where the time goes in v7:
time: 376 us; the launch traced here: 375 us
  waiting for transfers between devices  290 us (77%)
  Pallas kernels  44.9 us (12%)
  between operations  14.8 us (4%)
  other arithmetic  12.5 us (3%)
  local copies, waits for them, and re-layouts  11.9 us (3%)
    reduce_scatter x1, waiting for transfers between devices, shards(): lax.psum_scatter(partial_cols, 'wide', scatter_dimension=0, tiled=True)  90.4 us
    reduce_scatter x2, waiting for transfers between devices, shards(): lax.psum_scatter(partial_rows, 'narrow', scatter_dimension=0, tiled=True)  86.1 us
    all_gather x1, waiting for transfers between devices, shards(): yb = lax.all_gather(y_cols.astype(jnp.bfloat16), 'wide', axis=0, tiled=True)  58.2 us
    pallas_call x3, Pallas kernels, sweep(): pl.pallas_call(functools.partial(sweep_kernel, want_rows, echo, tile), gr...  44.9 us
    all_gather x1, waiting for transfers between devices, shards(): x_now = lax.all_gather(x_mine, 'narrow', axis=0, tiled=True)  30.9 us
    all_gather x1, waiting for transfers between devices, shards(): lax.all_gather(x_mine.astype(jnp.bfloat16), 'narrow', axis=0, tiled=True)  24.4 us
    unnamed x5, local copies, waits for them, and re-layouts  11.9 us
  transfers between devices with their start and end apart: 6, of which 6 were waited for; matrix products, arithmetic and copies ran while one was open for 4% of the time, Pallas kernels for 0%

profile of v7, /device:TPU:0, one launch (start us, length us, event | category | flops | bytes accessed | tf_op | source)
XLA Modules:
  0.0 374.7 jit_solution(16784871565782571314)
XLA Ops:
  7.2 0.0 all-gather.4.cloned.1.call-start
  7.2 2.1 convert_element_type.13
  9.3 0.0 all-gather.4.cloned.1.call-update
  9.3 0.0 reduce-scatter.4.cloned.1.call-start
  10.0 3.7 convert_element_type.12.x_ref
  13.7 11.9 %copy.8 = bf16[1,1,256,128,128]{3,4,2,1,0:T(8,128)(2,1)} copy(bf16[1,1,256,128,128]{4,3,2,1,0:T(8,128)(2,1)} %param.8) | data formatting | bytes 16777216 | tf_op args[2]
  25.6 58.2 %all-gather.4.cloned.1.call-done.y_ref = bf16[16384,256]{1,0:T(8,128)(2,1)} async-done(((bf16[1024,256]{1,0:T(8,128)(2,1)}), bf16[16384,256]{1,0:T(8,128)(2,1)}) %all-gather.4.cloned.1.call-update) | async-done | bytes 8388624 | tf_op jit(solution)/shard_map/all_gather | solution.py:111
  83.9 13.3 %shard_map.77 = f32[4096,256]{1,0:T(8,128)} custom-call(s32[256]{0:T(256)} %bitcast.14, s32[256]{0:T(256)} %bitcast.17, s32[1]{0:T(128)} %bitcast.7.cnt_ref, bf16[4096,256]{1,0:T(8,128)(2,1)} %convert_element_type.12.x_ref, bf16[16384,256]{1,0:T(8,128)(2,1)} %all-gather.4.cloned.1.call-done.y_ref, bf16[256,128,128]{2,1,0:T(8,128)(2,1)} %bitcast.12, ...), custom_call_target="tpu_custom_call" | custom-call | flops 4294967296 | bytes 20971520 | tf_op jit(solution)/shard_map/pallas_call | solution.py:94
  97.1 0.0 reduce-scatter.4.cloned.1.call-update
  97.2 0.0 all-gather.6.cloned.1.call-start
  97.2 42.9 %reduce-scatter.4.cloned.1.call-done = f32[512,256]{1,0:T(8,128)} async-done(((f32[4096,256]{1,0:T(8,128)}), f32[512,256]{1,0:T(8,128)}) %reduce-scatter.4.cloned.1.call-update) | async-done | bytes 524304 | tf_op jit(solution)/shard_map/reduce_scatter | solution.py:123
  140.2 2.1 fusion
  142.3 0.0 all-gather.6.cloned.1.call-update
  142.3 0.0 reduce-scatter.6.cloned.1.call-start
  142.4 24.4 %all-gather.6.cloned.1.call-done.x_ref = bf16[4096,256]{1,0:T(8,128)(2,1)} async-done(((bf16[512,256]{1,0:T(8,128)(2,1)}), bf16[4096,256]{1,0:T(8,128)(2,1)}) %all-gather.6.cloned.1.call-update) | async-done | bytes 2097168 | tf_op jit(solution)/shard_map/all_gather | solution.py:125
  166.7 13.3 %shard_map.78 = f32[4096,256]{1,0:T(8,128)} custom-call(s32[256]{0:T(256)} %bitcast.15, s32[256]{0:T(256)} %bitcast.18, s32[1]{0:T(128)} %bitcast.8.cnt_ref, bf16[4096,256]{1,0:T(8,128)(2,1)} %all-gather.6.cloned.1.call-done.x_ref, bf16[16384,256]{1,0:T(8,128)(2,1)} %all-gather.4.cloned.1.call-done.y_ref, bf16[256,128,128]{2,1,0:T(8,128)(2,1)} %bitcast.13), custom_call_target="tpu_custom_call" | custom-call | flops 4294967296 | bytes 20971520 | tf_op jit(solution)/shard_map/pallas_call | solution.py:94
  180.0 0.0 copy-start.1
  180.0 0.0 reduce-scatter.6.cloned.1.call-update
  180.0 0.0 all-gather.8.cloned.1.call-start
  180.1 43.2 %reduce-scatter.6.cloned.1.call-done = f32[512,256]{1,0:T(8,128)} async-done(((f32[4096,256]{1,0:T(8,128)}), f32[512,256]{1,0:T(8,128)}) %reduce-scatter.6.cloned.1.call-update) | async-done | bytes 524304 | tf_op jit(solution)/shard_map/reduce_scatter | solution.py:128
  223.2 0.0 copy-done.1
  223.2 2.4 maximum_multiply_fusion
  225.7 0.0 all-gather.8.cloned.1.call-update
  225.7 0.2 reduce-scatter.8.cloned.1.call-start
  225.9 30.9 %all-gather.8.cloned.1.call-done.x_ref = f32[4096,256]{1,0:T(8,128)} async-done(((f32[512,256]{1,0:T(8,128)}), f32[4096,256]{1,0:T(8,128)}) %all-gather.8.cloned.1.call-update) | async-done | bytes 4194320 | tf_op jit(solution)/shard_map/all_gather | solution.py:130
  256.9 18.4 %shard_map.79 = (bf16[16384,256]{1,0:T(8,128)(2,1)}, f32[4096,256]{1,0:T(8,128)}) custom-call(s32[256]{0:T(256)} %bitcast.16, s32[256]{0:T(256)} %bitcast.19, s32[1]{0:T(128)} %bitcast.9.cnt_ref, f32[4096,256]{1,0:T(8,128)} %all-gather.8.cloned.1.call-done.x_ref, bf16[16384,256]{1,0:T(8,128)(2,1)} %all-gather.4.cloned.1.call-done.y_ref, ...), custom_call_target="tpu_custom_call" | custom-call | flops 4294967296 | bytes 29360128 | tf_op jit(solution)/shard_map/pallas_call | solution.py:94
  275.3 0.0 copy-start
  275.3 0.0 reduce-scatter.8.cloned.1.call-update
  275.3 90.4 %reduce-scatter.8.cloned.1.call-done = bf16[1024,256]{1,0:T(8,128)(2,1)} async-done(((bf16[16384,256]{1,0:T(8,128)(2,1)}), bf16[1024,256]{1,0:T(8,128)(2,1)}) %reduce-scatter.8.cloned.1.call-update) | async-done | bytes 524304 | tf_op jit(solution)/shard_map/reduce_scatter | solution.py:133
  365.7 0.0 copy-done
  365.7 2.1 multiply_subtract_fusion
Async XLA Ops:
  7.2 76.7 %all-gather.4.cloned.1.call-start = ((), (), s32[]{:S(2)}) async-start(), calls=%async_computation.3 | async-start | bytes 8912896 | tf_op jit(solution)/shard_map/all_gather | solution.py:111
  9.3 130.8 %reduce-scatter.4.cloned.1.call-start = ((), (), s32[]{:S(2)}) async-start(), calls=%async_computation.4 | async-start | bytes 4718592 | tf_op jit(solution)/shard_map/reduce_scatter | solution.py:123
  97.2 69.6 %all-gather.6.cloned.1.call-start = ((), (), s32[]{:S(2)}) async-start(), calls=%async_computation.5 | async-start | bytes 2359296 | tf_op jit(solution)/shard_map/all_gather | solution.py:125
  142.3 80.9 %reduce-scatter.6.cloned.1.call-start = ((), (), s32[]{:S(2)}) async-start(), calls=%async_computation.6 | async-start | bytes 4718592 | tf_op jit(solution)/shard_map/reduce_scatter | solution.py:128
  180.0 43.3 %copy-start.1 = (f32[512,256]{1,0:T(8,128)S(1)}, f32[512,256]{1,0:T(8,128)}, u32[]{:S(2)}) copy-start(f32[512,256]{1,0:T(8,128)} %reduce-scatter.4.cloned.1.call-done) | copy-start | bytes 1572868
  180.0 76.8 %all-gather.8.cloned.1.call-start = ((), (), s32[]{:S(2)}) async-start(), calls=%async_computation.7 | async-start | bytes 4718592 | tf_op jit(solution)/shard_map/all_gather | solution.py:130
  225.7 140.0 %reduce-scatter.8.cloned.1.call-start = ((), (), s32[]{:S(2)}) async-start(), calls=%async_computation.8 | async-start | bytes 8912896 | tf_op jit(solution)/shard_map/reduce_scatter | solution.py:133
  275.3 90.5 %copy-start = (f32[1024,256]{1,0:T(8,128)S(1)}, f32[1024,256]{1,0:T(8,128)}, u32[]{:S(2)}) copy-start(f32[1024,256]{1,0:T(8,128)} %param.7) | copy-start | bytes 3145732
Sparse Core Ops, SparseCore 0:
  10.7 73.1 all-gather.3
  97.3 42.8 reduce-scatter.3
  142.5 24.2 all-gather.5
  180.1 43.0 reduce-scatter.5
  225.8 30.9 all-gather.7
  275.4 90.2 reduce-scatter.7

commit v8 on v7

--- a/solution.py
+++ b/solution.py
@@ -35,8 +35,7 @@
             echo_ref[...] = x_ref[...]
             xbuf[...] = x_ref[...].astype(jnp.bfloat16)
 
-    @pl.when(step * BATCH < count)
-    def _():
+    def run(masked):
         parts = []
         for j in range(BATCH):
             s = step * BATCH + j
@@ -47,14 +46,28 @@
             vals = v_ref[j].astype(jnp.float32)
             if want_rows:
                 pred = lax.dot_general(xs, ys, (((1,), (1,)), ((), ())), preferred_element_type=jnp.float32)
-                slope = jnp.where(s < count, jnp.clip(pred - vals, -huber_delta, huber_delta), 0.0).astype(jnp.bfloat16)
+            else:
+                pred = lax.dot_general(ys, xs, (((1,), (1,)), ((), ())), preferred_element_type=jnp.float32)
+            slope = jnp.clip(pred - vals, -huber_delta, huber_delta)
+            if masked:
+                slope = jnp.where(s < count, slope, 0.0)
+            slope = slope.astype(jnp.bfloat16)
+            if want_rows:
                 parts.append((r0, jnp.dot(slope, ys, preferred_element_type=jnp.float32)))
             else:
-                pred_t = lax.dot_general(ys, xs, (((1,), (1,)), ((), ())), preferred_element_type=jnp.float32)
-                slope_t = jnp.where(s < count, jnp.clip(pred_t - vals, -huber_delta, huber_delta), 0.0).astype(jnp.bfloat16)
-                parts.append((c0, jnp.dot(slope_t, xs, preferred_element_type=jnp.float32)))
+                parts.append((c0, jnp.dot(slope, xs, preferred_element_type=jnp.float32)))
         for o0, contrib in parts:
             acc_ref[pl.ds(o0, tile), :] += contrib
+
+    full = (step + 1) * BATCH <= count
+
+    @pl.when(full)
+    def _():
+        run(False)
+
+    @pl.when(jnp.logical_and(jnp.logical_not(full), step * BATCH < count))
+    def _():
+        run(True)
 
     @pl.when(step == pl.num_programs(0) - 1)
     def _():

time: 376 us -> 376 us (level)
  waiting for transfers between devices: 290 us -> 274 us
  Pallas kernels: 44.9 us -> 60.5 us
    pallas_call x3, Pallas kernels: 44.9 us -> 60.5 us  [sweep(): pl.pallas_call(functools.partial(sweep_kernel, want_rows, echo, tile), gr...]
    reduce_scatter x2, waiting for transfers between devices: 86.1 us -> 75.3 us  [shards(): lax.psum_scatter(partial_rows, 'narrow', scatter_dimension=0, tiled=True)]
    reduce_scatter x1, waiting for transfers between devices: 90.4 us -> 84.9 us  [shards(): lax.psum_scatter(partial_cols, 'wide', scatter_dimension=0, tiled=True)]
where the time goes in v8:
time: 376 us; the launch traced here: 374 us
  waiting for transfers between devices  274 us (73%)
  Pallas kernels  60.5 us (16%)
  between operations  14.8 us (4%)
  other arithmetic  12.5 us (3%)
  local copies, waits for them, and re-layouts  11.9 us (3%)
    reduce_scatter x1, waiting for transfers between devices, shards(): lax.psum_scatter(partial_cols, 'wide', scatter_dimension=0, tiled=True)  84.9 us
    reduce_scatter x2, waiting for transfers between devices, shards(): lax.psum_scatter(partial_rows, 'narrow', scatter_dimension=0, tiled=True)  75.3 us
    pallas_call x3, Pallas kernels, sweep(): pl.pallas_call(functools.partial(sweep_kernel, want_rows, echo, tile), gr...  60.5 us
    all_gather x1, waiting for transfers between devices, shards(): yb = lax.all_gather(y_cols.astype(jnp.bfloat16), 'wide', axis=0, tiled=True)  58.2 us
    all_gather x1, waiting for transfers between devices, shards(): x_now = lax.all_gather(x_mine, 'narrow', axis=0, tiled=True)  30.9 us
    all_gather x1, waiting for transfers between devices, shards(): lax.all_gather(x_mine.astype(jnp.bfloat16), 'narrow', axis=0, tiled=True)  24.2 us
    unnamed x5, local copies, waits for them, and re-layouts  11.9 us
  transfers between devices with their start and end apart: 6, of which 6 were waited for; matrix products, arithmetic and copies ran while one was open for 4% of the time, Pallas kernels for 0%

profile of v8, /device:TPU:0, one launch (start us, length us, event | category | flops | bytes accessed | tf_op | source)
XLA Modules:
  0.0 373.9 jit_solution(3757134054097347809)
XLA Ops:
  7.2 0.0 all-gather.4.cloned.1.call-start
  7.2 2.1 convert_element_type.13
  9.3 0.0 all-gather.4.cloned.1.call-update
  9.3 0.0 reduce-scatter.4.cloned.1.call-start
  10.0 3.7 convert_element_type.12.x_ref
  13.7 11.9 %copy.8 = bf16[1,1,256,128,128]{3,4,2,1,0:T(8,128)(2,1)} copy(bf16[1,1,256,128,128]{4,3,2,1,0:T(8,128)(2,1)} %param.8) | data formatting | bytes 16777216 | tf_op args[2]
  25.6 58.2 %all-gather.4.cloned.1.call-done.y_ref = bf16[16384,256]{1,0:T(8,128)(2,1)} async-done(((bf16[1024,256]{1,0:T(8,128)(2,1)}), bf16[16384,256]{1,0:T(8,128)(2,1)}) %all-gather.4.cloned.1.call-update) | async-done | bytes 8388624 | tf_op jit(solution)/shard_map/all_gather | solution.py:124
  83.9 18.4 %shard_map.77 = f32[4096,256]{1,0:T(8,128)} custom-call(s32[256]{0:T(256)} %bitcast.14, s32[256]{0:T(256)} %bitcast.17, s32[1]{0:T(128)} %bitcast.7.cnt_ref, bf16[4096,256]{1,0:T(8,128)(2,1)} %convert_element_type.12.x_ref, bf16[16384,256]{1,0:T(8,128)(2,1)} %all-gather.4.cloned.1.call-done.y_ref, bf16[256,128,128]{2,1,0:T(8,128)(2,1)} %bitcast.12, ...), custom_call_target="tpu_custom_call" | custom-call | flops 4294967296 | bytes 20971520 | tf_op jit(solution)/shard_map/pallas_call | solution.py:107
  102.3 0.0 reduce-scatter.4.cloned.1.call-update
  102.3 0.0 all-gather.6.cloned.1.call-start
  102.4 37.4 %reduce-scatter.4.cloned.1.call-done = f32[512,256]{1,0:T(8,128)} async-done(((f32[4096,256]{1,0:T(8,128)}), f32[512,256]{1,0:T(8,128)}) %reduce-scatter.4.cloned.1.call-update) | async-done | bytes 524304 | tf_op jit(solution)/shard_map/reduce_scatter | solution.py:136
  139.8 2.1 fusion
  141.9 0.0 all-gather.6.cloned.1.call-update
  142.0 0.2 reduce-scatter.6.cloned.1.call-start
  142.2 24.2 %all-gather.6.cloned.1.call-done.x_ref = bf16[4096,256]{1,0:T(8,128)(2,1)} async-done(((bf16[512,256]{1,0:T(8,128)(2,1)}), bf16[4096,256]{1,0:T(8,128)(2,1)}) %all-gather.6.cloned.1.call-update) | async-done | bytes 2097168 | tf_op jit(solution)/shard_map/all_gather | solution.py:138
  166.4 18.4 %shard_map.78 = f32[4096,256]{1,0:T(8,128)} custom-call(s32[256]{0:T(256)} %bitcast.15, s32[256]{0:T(256)} %bitcast.18, s32[1]{0:T(128)} %bitcast.8.cnt_ref, bf16[4096,256]{1,0:T(8,128)(2,1)} %all-gather.6.cloned.1.call-done.x_ref, bf16[16384,256]{1,0:T(8,128)(2,1)} %all-gather.4.cloned.1.call-done.y_ref, bf16[256,128,128]{2,1,0:T(8,128)(2,1)} %bitcast.13), custom_call_target="tpu_custom_call" | custom-call | flops 4294967296 | bytes 20971520 | tf_op jit(solution)/shard_map/pallas_call | solution.py:107
  184.8 0.0 copy-start.1
  184.8 0.0 reduce-scatter.6.cloned.1.call-update
  184.9 0.0 all-gather.8.cloned.1.call-start
  184.9 37.8 %reduce-scatter.6.cloned.1.call-done = f32[512,256]{1,0:T(8,128)} async-done(((f32[4096,256]{1,0:T(8,128)}), f32[512,256]{1,0:T(8,128)}) %reduce-scatter.6.cloned.1.call-update) | async-done | bytes 524304 | tf_op jit(solution)/shard_map/reduce_scatter | solution.py:141
  222.8 0.0 copy-done.1
  222.8 2.4 maximum_multiply_fusion
  225.2 0.0 all-gather.8.cloned.1.call-update
  225.2 0.3 reduce-scatter.8.cloned.1.call-start
  225.5 30.9 %all-gather.8.cloned.1.call-done.x_ref = f32[4096,256]{1,0:T(8,128)} async-done(((f32[512,256]{1,0:T(8,128)}), f32[4096,256]{1,0:T(8,128)}) %all-gather.8.cloned.1.call-update) | async-done | bytes 4194320 | tf_op jit(solution)/shard_map/all_gather | solution.py:143
  256.4 23.6 %shard_map.79 = (bf16[16384,256]{1,0:T(8,128)(2,1)}, f32[4096,256]{1,0:T(8,128)}) custom-call(s32[256]{0:T(256)} %bitcast.16, s32[256]{0:T(256)} %bitcast.19, s32[1]{0:T(128)} %bitcast.9.cnt_ref, f32[4096,256]{1,0:T(8,128)} %all-gather.8.cloned.1.call-done.x_ref, bf16[16384,256]{1,0:T(8,128)(2,1)} %all-gather.4.cloned.1.call-done.y_ref, ...), custom_call_target="tpu_custom_call" | custom-call | flops 4294967296 | bytes 29360128 | tf_op jit(solution)/shard_map/pallas_call | solution.py:107
  280.0 0.0 copy-start
  280.0 0.0 reduce-scatter.8.cloned.1.call-update
  280.0 84.9 %reduce-scatter.8.cloned.1.call-done = bf16[1024,256]{1,0:T(8,128)(2,1)} async-done(((bf16[16384,256]{1,0:T(8,128)(2,1)}), bf16[1024,256]{1,0:T(8,128)(2,1)}) %reduce-scatter.8.cloned.1.call-update) | async-done | bytes 524304 | tf_op jit(solution)/shard_map/reduce_scatter | solution.py:146
  364.9 0.0 copy-done
  364.9 2.1 multiply_subtract_fusion
Async XLA Ops:
  7.2 76.7 %all-gather.4.cloned.1.call-start = ((), (), s32[]{:S(2)}) async-start(), calls=%async_computation.3 | async-start | bytes 8912896 | tf_op jit(solution)/shard_map/all_gather | solution.py:124
  9.3 130.5 %reduce-scatter.4.cloned.1.call-start = ((), (), s32[]{:S(2)}) async-start(), calls=%async_computation.4 | async-start | bytes 4718592 | tf_op jit(solution)/shard_map/reduce_scatter | solution.py:136
  102.3 64.1 %all-gather.6.cloned.1.call-start = ((), (), s32[]{:S(2)}) async-start(), calls=%async_computation.5 | async-start | bytes 2359296 | tf_op jit(solution)/shard_map/all_gather | solution.py:138
  142.0 80.8 %reduce-scatter.6.cloned.1.call-start = ((), (), s32[]{:S(2)}) async-start(), calls=%async_computation.6 | async-start | bytes 4718592 | tf_op jit(solution)/shard_map/reduce_scatter | solution.py:141
  184.8 37.9 %copy-start.1 = (f32[512,256]{1,0:T(8,128)S(1)}, f32[512,256]{1,0:T(8,128)}, u32[]{:S(2)}) copy-start(f32[512,256]{1,0:T(8,128)} %reduce-scatter.4.cloned.1.call-done) | copy-start | bytes 1572868
  184.9 71.5 %all-gather.8.cloned.1.call-start = ((), (), s32[]{:S(2)}) async-start(), calls=%async_computation.7 | async-start | bytes 4718592 | tf_op jit(solution)/shard_map/all_gather | solution.py:143
  225.2 139.7 %reduce-scatter.8.cloned.1.call-start = ((), (), s32[]{:S(2)}) async-start(), calls=%async_computation.8 | async-start | bytes 8912896 | tf_op jit(solution)/shard_map/reduce_scatter | solution.py:146
  280.0 85.0 %copy-start = (f32[1024,256]{1,0:T(8,128)S(1)}, f32[1024,256]{1,0:T(8,128)}, u32[]{:S(2)}) copy-start(f32[1024,256]{1,0:T(8,128)} %param.7) | copy-start | bytes 3145732
Sparse Core Ops, SparseCore 0:
  10.7 73.1 all-gather.3
  102.4 37.3 reduce-scatter.3
  142.1 24.2 all-gather.5
  185.0 37.7 reduce-scatter.5
  225.3 30.9 all-gather.7
  280.1 84.7 reduce-scatter.7
